TPU v7x, 512 devices: a whole 4x8x8 slice. The times are simulated.
512 devices in a mesh: band: 128 (over x, z_hi, y, core), depth: 4 (over z_lo).
Axes of the slice: x: 4, y: 8, z: 8 (z_hi: 2, z_lo: 4; z = z_hi * 4 + z_lo), core: 2. Of those that a mesh axis runs over, the one named last changes fastest.
Arguments:
- orbitals: bfloat16 [128, 32, 128, 128], P('band', 'depth'), may hold values from -6 to 6
- dielectric: float32 [32, 128, 128], P('depth'), may hold values from 1 to 4
- occupied: int32 [128], P('band'), may hold values 0 or 1
- plan: int32 [2, 128, 1], P(None, 'band'), may hold values 0 or 1
Outputs:
- exchange: float32 [128, 32, 128, 128], P('band', 'depth')
All inputs are finite; a program needn't handle non-finite values. No bound on the sum of `occupied` or of `plan` on one device may be relied on, other than what follows from the above.
Results may differ from a plain program's by a relative error of at most 0.0003.
Values may be sent and summed in bfloat16 or wider, within the bound.
No kernel may reach another device: no remote copies, remote signals or barrier semaphores. Data moves between devices by JAX's collectives and lax.ppermute only.
A program may use at most 64 MiB of HBM per device.

v0:
```python
import math

import jax
import jax.numpy as jnp
from jax import lax
from jax.sharding import PartitionSpec as P

SWEEPS = 2


FOUR_PI = 4.0 * math.pi
KAPPA_SQ = 4.0
CHEB_CENTER = 28.0
CHEB_HALF = 24.0


def with_halo(x, sides, width):
    for axis, dim in sides:
        size, length = (lax.axis_size(axis), x.shape[dim])
        up = [(i, (i + 1) % size) for i in range(size)]
        down = [(j, i) for i, j in up]
        last = lax.slice_in_dim(x, length - width, length, axis=dim)
        leading = lax.slice_in_dim(x, 0, width, axis=dim)
        before = lax.ppermute(last, axis, up)
        after = lax.ppermute(leading, axis, down)
        x = jnp.concatenate([before, x, after], axis=dim)
    return x


def passed_along(x, axis, by):
    size = lax.axis_size(axis)
    return lax.ppermute(x, axis, [(i, (i + by) % size) for i in range(size)])


def face_tables(padded_diel):
    face_z = (padded_diel[:-1] + padded_diel[1:]) * 0.5
    face_x = (padded_diel + jnp.roll(padded_diel, -1, 1)) * 0.5
    face_y = (padded_diel + jnp.roll(padded_diel, -1, 2)) * 0.5
    return (face_z, face_x, face_y)


def stencil_apply(field, margin, faces):
    face_z, face_x, face_y = faces
    length = field.shape[2]
    coef_z = face_z[2 - margin : 2 - margin + length - 1]
    flux_z = coef_z * (field[:, :, 1:] - field[:, :, :-1])
    part_z = flux_z[:, :, 1:] - flux_z[:, :, :-1]
    center = field[:, :, 1:-1]
    coef_x = face_x[3 - margin : 3 - margin + length - 2]
    coef_y = face_y[3 - margin : 3 - margin + length - 2]
    flux_x = coef_x * (jnp.roll(center, -1, 3) - center)
    part_x = flux_x - jnp.roll(flux_x, 1, 3)
    flux_y = coef_y * (jnp.roll(center, -1, 4) - center)
    part_y = flux_y - jnp.roll(flux_y, 1, 4)
    return KAPPA_SQ * center - (part_z + part_x + part_y)


def potential_of(source, faces):
    sigma = CHEB_CENTER / CHEB_HALF
    factor = CHEB_HALF / CHEB_CENTER
    direction = source / CHEB_CENTER
    solution = direction
    remainder = source
    for sweep in range(SWEEPS):
        widened = with_halo(direction, (("depth", 2),), 1)
        remainder = remainder - stencil_apply(widened, 1, faces)
        factor_next = 1.0 / (2.0 * sigma - factor)
        direction = factor_next * factor * direction + 2.0 * factor_next / CHEB_HALF * remainder
        solution = solution + direction
        factor = factor_next
    return solution


def advance_visitors(visitor, visitor_occ):
    return passed_along((visitor, visitor_occ), "band", 1)


def on_device(orbitals, dielectric, occupied, plan):
    ticks = plan.shape[0]
    padded_diel = with_halo(dielectric, (("depth", 0),), 2)
    faces = face_tables(padded_diel)
    own_wide = orbitals.astype(jnp.float32)
    own_occ = occupied.astype(jnp.float32)
    weights = plan.astype(jnp.float32)
    totals = jnp.zeros(own_wide.shape, jnp.float32)
    visitor = orbitals
    visitor_occ = occupied.astype(jnp.bfloat16)
    carried_sum = jnp.zeros(own_wide.shape, jnp.float32)
    for tick in range(ticks):
        visitor, visitor_occ = advance_visitors(visitor, visitor_occ)
        if tick > 0:
            carried_sum = passed_along(carried_sum, "band", 1)
        partner = visitor.astype(jnp.float32)
        potential = potential_of(FOUR_PI * own_wide[:, None] * partner[None, :], faces)
        coef_own = weights[tick] * visitor_occ.astype(jnp.float32)[None, :]
        totals = totals + jnp.sum(
            coef_own[:, :, None, None, None] * potential * partner[None, :], axis=1
        )
        coef_back = weights[tick] * own_occ[:, None]
        carried_sum = carried_sum + jnp.sum(
            coef_back[:, :, None, None, None] * potential * own_wide[:, None], axis=0
        )
    totals = totals + passed_along(carried_sum, "band", -ticks)
    return -totals


def solution(mesh):
    placed = (
        P("band", "depth", None, None),
        P("depth", None, None),
        P("band"),
        P(None, "band", None),
    )
    return jax.shard_map(
        on_device,
        mesh=mesh,
        in_specs=placed,
        out_specs=P("band", "depth", None, None),
        check_vma=False,
    )
```

profile of v0, /device:TPU:64, one launch (start us, length us, event | category | flops | bytes accessed | tf_op | source)
XLA Modules:
  0.0 165.4 jit_solution(6763565982750539738)
XLA Ops:
  0.0 1.3 copy.40
  1.5 4.3 %collective-permute-start.2 = (f32[2,128,128]{2,0,1:T(2,128)S(1)}, f32[2,128,128]{2,0,1:T(2,128)S(1)}, u32[]{:S(2)}, u32[]{:S(2)}) collective-permute-start(f32[2,128,128]{2,0,1:T(2,128)S(1)} %get-tuple-element.39), channel_id=1, source_target_pairs={{0,1},{1,2},{2,3},{3,0},{4,5},{5,6},{6,7},{7,4},{8,9},{9,10},{10,1... | collective-permute-start | bytes 393224 | tf_op jit(solution)/shard_map/ppermute | solution.py:24
  5.8 4.5 %collective-permute-start.3 = (f32[2,128,128]{2,0,1:T(2,128)S(1)}, f32[2,128,128]{2,0,1:T(2,128)S(1)}, u32[]{:S(2)}, u32[]{:S(2)}) collective-permute-start(f32[2,128,128]{2,0,1:T(2,128)S(1)} %get-tuple-element.40), channel_id=1, source_target_pairs={{1,0},{2,1},{3,2},{0,3},{5,4},{6,5},{7,6},{4,7},{9,8},{10,9},{11,1... | collective-permute-start | bytes 393224 | tf_op jit(solution)/shard_map/ppermute | solution.py:25
  10.5 1.9 %collective-permute-start.1 = (bf16[1,8,128,128]{3,1,2,0:T(8,128)(2,1)S(1)}, bf16[1,8,128,128]{3,1,2,0:T(8,128)(2,1)S(1)}, u32[]{:S(2)}, u32[]{:S(2)}) collective-permute-start(bf16[1,8,128,128]{3,1,2,0:T(8,128)(2,1)S(1)} %copy.38), channel_id=1, source_target_pairs={{0,4},{4,8},{8,12},{12,16},{16,20},{20,24},{24,28},{28,32},{32,36}... | collective-permute-start | bytes 786440 | tf_op jit(solution)/shard_map/ppermute | solution.py:32
  14.8 1.4 slice.300
  17.2 10.7 %collective-permute-done.1 = bf16[1,8,128,128]{3,1,2,0:T(8,128)(2,1)S(1)} collective-permute-done((bf16[1,8,128,128]{3,1,2,0:T(8,128)(2,1)S(1)}, bf16[1,8,128,128]{3,1,2,0:T(8,128)(2,1)S(1)}, u32[]{:S(2)}, u32[]{:S(2)}) %collective-permute-start.1) | collective-permute-done | bytes 262176 | tf_op jit(solution)/shard_map/ppermute | solution.py:32
  28.0 1.9 %collective-permute-start.9 = (bf16[1,8,128,128]{3,1,2,0:T(8,128)(2,1)S(1)}, bf16[1,8,128,128]{3,1,2,0:T(8,128)(2,1)S(1)}, u32[]{:S(2)}, u32[]{:S(2)}) collective-permute-start(bf16[1,8,128,128]{3,1,2,0:T(8,128)(2,1)S(1)} %collective-permute-done.1), channel_id=1, source_target_pairs={{0,4},{4,8},{8,12},{12,16},{16,20},{20,24},{24,28},{28,32},{32,36}... | collective-permute-start | bytes 786440 | tf_op jit(solution)/shard_map/ppermute | solution.py:32
  29.9 1.5 fusion.76
  31.3 14.7 %collective-permute-done.9 = bf16[1,8,128,128]{3,1,2,0:T(8,128)(2,1)S(1)} collective-permute-done((bf16[1,8,128,128]{3,1,2,0:T(8,128)(2,1)S(1)}, bf16[1,8,128,128]{3,1,2,0:T(8,128)(2,1)S(1)}, u32[]{:S(2)}, u32[]{:S(2)}) %collective-permute-start.9) | collective-permute-done | bytes 262176 | tf_op jit(solution)/shard_map/ppermute | solution.py:32
  49.4 2.5 %fusion.65 = (f32[1,1,8,128,128]{4,2,3,1,0:T(8,128)S(1)}, f32[8,128,128]{2,0,1:T(8,128)S(1)}, f32[1,1,8,128,128]{4,2,3,1,0:T(8,128)S(1)}, f32[8,128,128]{2,0,1:T(8,128)S(1)}) fusion(f32[8,1,128]{2,0,1:T(8,128)S(1)} %slice_bitcast_fusion.9, f32[8,127,128]{2,0,1:T(8,128)} %slice_bitcast_fusion.5, bf16[1,8,128,128]{3,1,2,0:T(8,128)(2,1)S(1)} %collective-permute-done.9, ...), kind=kLoop, calls=%fused_computation.115 | loop fusion | flops 2228224 | bytes 5767168 | tf_op jit(solution)/shard_map/mul | solution.py:51
  53.6 5.3 %collective-permute-start.10 = (f32[1,1,1,128,128]{4,2,3,1,0:T(1,128)}, f32[1,1,1,128,128]{4,2,3,1,0:T(1,128)S(1)}, u32[]{:S(2)}, u32[]{:S(2)}) collective-permute-start(f32[1,1,1,128,128]{4,2,3,1,0:T(1,128)} %get-tuple-element.36), channel_id=1, source_target_pairs={{1,0},{2,1},{3,2},{0,3},{5,4},{6,5},{7,6},{4,7},{9,8},{10,9},{11,1... | collective-permute-start | bytes 196616 | tf_op jit(solution)/shard_map/ppermute | solution.py:25
  58.9 1.9 %collective-permute-start.11 = (f32[1,1,1,128,128]{4,2,3,1,0:T(1,128)S(1)}, f32[1,1,1,128,128]{4,2,3,1,0:T(1,128)S(1)}, u32[]{:S(2)}, u32[]{:S(2)}) collective-permute-start(f32[1,1,1,128,128]{4,2,3,1,0:T(1,128)S(1)} %copy-done.23), channel_id=1, source_target_pairs={{0,1},{1,2},{2,3},{3,0},{4,5},{5,6},{6,7},{7,4},{8,9},{9,10},{10,1... | collective-permute-start | bytes 196616 | tf_op jit(solution)/shard_map/ppermute | solution.py:24
  63.6 2.1 %collective-permute-done.11 = f32[1,1,1,128,128]{4,2,3,1,0:T(1,128)S(1)} collective-permute-done((f32[1,1,1,128,128]{4,2,3,1,0:T(1,128)S(1)}, f32[1,1,1,128,128]{4,2,3,1,0:T(1,128)S(1)}, u32[]{:S(2)}, u32[]{:S(2)}) %collective-permute-start.11) | collective-permute-done | bytes 65568 | tf_op jit(solution)/shard_map/ppermute | solution.py:24
  65.8 2.1 %fusion.6 = (f32[1,1,9,128,128]{4,2,3,1,0:T(8,128)S(1)}, f32[9,128,128]{2,0,1:T(8,128)S(1)}) fusion(f32[1,128,128]{2,0,1:T(1,128)S(1)} %bitcast.241, f32[8,128,128]{2,0,1:T(8,128)} %get-tuple-element.43, f32[1,128,128]{2,0,1:T(1,128)S(1)} %bitcast.242, f32[11,128,128]{2,0,1:T(8,128)} %get-tuple-element.24, f32[11,128,128]{2,0,1:T(8,128)S(1)} %copy-done.14), kind=kLoop, calls=%fused_computation.11 | loop fusion | flops 884736 | bytes 3014656 | tf_op jit(solution)/shard_map/mul | solution.py:46
  68.3 1.5 multiply_add_fusion
  72.6 3.1 %collective-permute-start.4 = (f32[1,1,1,128,128]{4,3,2,1,0:T(8,128)}, f32[1,1,1,128,128]{4,3,2,1,0:T(8,128)S(1)}, u32[]{:S(2)}, u32[]{:S(2)}) collective-permute-start(f32[1,1,1,128,128]{4,3,2,1,0:T(8,128)} %bitcast.63), channel_id=1, source_target_pairs={{1,0},{2,1},{3,2},{0,3},{5,4},{6,5},{7,6},{4,7},{9,8},{10,9},{11,1... | collective-permute-start | bytes 196616 | tf_op jit(solution)/shard_map/ppermute | solution.py:25
  75.6 2.8 %collective-permute-start.5 = (f32[1,1,1,128,128]{4,3,2,1,0:T(8,128)}, f32[1,1,1,128,128]{4,3,2,1,0:T(8,128)S(1)}, u32[]{:S(2)}, u32[]{:S(2)}) collective-permute-start(f32[1,1,1,128,128]{4,3,2,1,0:T(8,128)} %bitcast.64), channel_id=1, source_target_pairs={{0,1},{1,2},{2,3},{3,0},{4,5},{5,6},{6,7},{7,4},{8,9},{9,10},{10,1... | collective-permute-start | bytes 196616 | tf_op jit(solution)/shard_map/ppermute | solution.py:24
  79.7 1.7 %fusion.66 = (f32[1,1,8,128,128]{4,2,3,1,0:T(8,128)S(1)}, f32[1,1,8,128,128]{4,2,3,1,0:T(8,128)S(1)}) fusion(f32[8,128,128]{2,0,1:T(8,128)S(1)} %get-tuple-element.12, f32[8,1,128]{2,0,1:T(8,128)S(1)} %slice_bitcast_fusion.11, f32[8,127,128]{2,0,1:T(8,128)} %slice_bitcast_fusion.7, bf16[1,8,128,128]{3,1,2,0:T(8,128)(2,1)S(1)} %copy-done.6, ...), kind=kLoop, calls=%fused_computation.116 | loop fusion | flops 1441792 | bytes 3670016 | tf_op jit(solution)/shard_map/mul | solution.py:51
  88.2 3.1 %collective-permute-start.12 = (f32[1,1,1,128,128]{4,3,2,1,0:T(8,128)}, f32[1,1,1,128,128]{4,3,2,1,0:T(8,128)S(1)}, u32[]{:S(2)}, u32[]{:S(2)}) collective-permute-start(f32[1,1,1,128,128]{4,3,2,1,0:T(8,128)} %bitcast.69), channel_id=1, source_target_pairs={{1,0},{2,1},{3,2},{0,3},{5,4},{6,5},{7,6},{4,7},{9,8},{10,9},{11,1... | collective-permute-start | bytes 196616 | tf_op jit(solution)/shard_map/ppermute | solution.py:25
  91.2 2.8 %collective-permute-start.13 = (f32[1,1,1,128,128]{4,3,2,1,0:T(8,128)}, f32[1,1,1,128,128]{4,3,2,1,0:T(8,128)S(1)}, u32[]{:S(2)}, u32[]{:S(2)}) collective-permute-start(f32[1,1,1,128,128]{4,3,2,1,0:T(8,128)} %bitcast.70), channel_id=1, source_target_pairs={{0,1},{1,2},{2,3},{3,0},{4,5},{5,6},{6,7},{7,4},{8,9},{9,10},{10,1... | collective-permute-start | bytes 196616 | tf_op jit(solution)/shard_map/ppermute | solution.py:24
  94.1 1.6 fusion.2
  96.0 1.7 %multiply_add_fusion.1 = (f32[1,1,8,128,128]{4,2,3,1,0:T(8,128)S(1)}, f32[1,1,8,128,128]{4,2,3,1,0:T(8,128)S(1)}) fusion(bf16[1,8,128,128]{3,1,2,0:T(8,128)(2,1)S(1)} %copy-done.6, bf16[1,8,128,128]{3,2,1,0:T(8,128)(2,1)S(1)} %copy-done, f32[8,128,127]{2,0,1:T(8,128)S(1)} %copy-done.16, f32[8,128,1]{2,0,1:T(8,128)S(1)} %copy-done.17, ...), kind=kLoop, calls=%fused_computation.104 | loop fusion | flops 3407872 | bytes 5767168 | tf_op jit(solution)/shard_map/add | solution.py:68
  98.1 3.5 %collective-permute-start.6 = (f32[1,1,1,128,128]{4,3,2,1,0:T(8,128)S(1)}, f32[1,1,1,128,128]{4,3,2,1,0:T(8,128)S(1)}, u32[]{:S(2)}, u32[]{:S(2)}) collective-permute-start(f32[1,1,1,128,128]{4,3,2,1,0:T(8,128)S(1)} %bitcast.246), channel_id=1, source_target_pairs={{1,0},{2,1},{3,2},{0,3},{5,4},{6,5},{7,6},{4,7},{9,8},{10,9},{11,1... | collective-permute-start | bytes 196616 | tf_op jit(solution)/shard_map/ppermute | solution.py:25
  101.7 2.4 %collective-permute-start.7 = (f32[1,1,1,128,128]{4,3,2,1,0:T(8,128)S(1)}, f32[1,1,1,128,128]{4,3,2,1,0:T(8,128)S(1)}, u32[]{:S(2)}, u32[]{:S(2)}) collective-permute-start(f32[1,1,1,128,128]{4,3,2,1,0:T(8,128)S(1)} %bitcast.245), channel_id=1, source_target_pairs={{0,1},{1,2},{2,3},{3,0},{4,5},{5,6},{6,7},{7,4},{8,9},{9,10},{10,1... | collective-permute-start | bytes 196616 | tf_op jit(solution)/shard_map/ppermute | solution.py:24
  104.9 4.7 %collective-permute-done.7 = f32[1,1,1,128,128]{4,3,2,1,0:T(8,128)S(1)} collective-permute-done((f32[1,1,1,128,128]{4,3,2,1,0:T(8,128)S(1)}, f32[1,1,1,128,128]{4,3,2,1,0:T(8,128)S(1)}, u32[]{:S(2)}, u32[]{:S(2)}) %collective-permute-start.7) | collective-permute-done | bytes 65568 | tf_op jit(solution)/shard_map/ppermute | solution.py:24
  110.7 1.9 %collective-permute-start.14 = (f32[1,8,128,128]{3,1,2,0:T(8,128)S(1)}, f32[1,8,128,128]{3,1,2,0:T(8,128)S(1)}, u32[]{:S(2)}, u32[]{:S(2)}) collective-permute-start(f32[1,8,128,128]{3,1,2,0:T(8,128)S(1)} %get-tuple-element.15), channel_id=1, source_target_pairs={{0,4},{4,8},{8,12},{12,16},{16,20},{20,24},{24,28},{28,32},{32,36}... | collective-permute-start | bytes 1572872 | tf_op jit(solution)/shard_map/ppermute | solution.py:32
  113.6 19.4 %collective-permute-done.14 = f32[1,8,128,128]{3,1,2,0:T(8,128)S(1)} collective-permute-done((f32[1,8,128,128]{3,1,2,0:T(8,128)S(1)}, f32[1,8,128,128]{3,1,2,0:T(8,128)S(1)}, u32[]{:S(2)}, u32[]{:S(2)}) %collective-permute-start.14) | collective-permute-done | bytes 524320 | tf_op jit(solution)/shard_map/ppermute | solution.py:32
  133.7 1.9 %collective-permute-start.15 = (f32[1,8,128,128]{3,1,2,0:T(8,128)S(1)}, f32[1,8,128,128]{3,1,2,0:T(8,128)S(1)}, u32[]{:S(2)}, u32[]{:S(2)}) collective-permute-start(f32[1,8,128,128]{3,1,2,0:T(8,128)S(1)} %get-tuple-element.5), channel_id=1, source_target_pairs={{0,504},{4,508},{8,0},{12,4},{16,8},{20,12},{24,16},{28,20},{32,24... | collective-permute-start | bytes 1572872 | tf_op jit(solution)/shard_map/ppermute | solution.py:32
  135.6 2.7 %collective-permute-start = (bf16[1]{0:T(256)(128)(2,1)}, bf16[1]{0:T(256)(128)(2,1)}, u32[]{:S(2)}, u32[]{:S(2)}) collective-permute-start(bf16[1]{0:T(256)(128)(2,1)} %convert_element_type.21), channel_id=1, source_target_pairs={{0,4},{4,8},{8,12},{12,16},{16,20},{20,24},{24,28},{28,32},{32,36}... | collective-permute-start | bytes 14 | tf_op jit(solution)/shard_map/ppermute | solution.py:32
  138.3 10.2 %collective-permute-done = bf16[1]{0:T(256)(128)(2,1)} collective-permute-done((bf16[1]{0:T(256)(128)(2,1)}, bf16[1]{0:T(256)(128)(2,1)}, u32[]{:S(2)}, u32[]{:S(2)}) %collective-permute-start) | collective-permute-done | bytes 34 | tf_op jit(solution)/shard_map/ppermute | solution.py:32
  149.9 1.9 %collective-permute-start.8 = (bf16[1]{0:T(256)(128)(2,1)}, bf16[1]{0:T(256)(128)(2,1)}, u32[]{:S(2)}, u32[]{:S(2)}) collective-permute-start(bf16[1]{0:T(256)(128)(2,1)} %collective-permute-done), channel_id=1, source_target_pairs={{0,4},{4,8},{8,12},{12,16},{16,20},{20,24},{24,28},{28,32},{32,36}... | collective-permute-start | bytes 14 | tf_op jit(solution)/shard_map/ppermute | solution.py:32
  151.8 11.2 %collective-permute-done.8 = bf16[1]{0:T(256)(128)(2,1)} collective-permute-done((bf16[1]{0:T(256)(128)(2,1)}, bf16[1]{0:T(256)(128)(2,1)}, u32[]{:S(2)}, u32[]{:S(2)}) %collective-permute-start.8) | collective-permute-done | bytes 34 | tf_op jit(solution)/shard_map/ppermute | solution.py:32
  (111 shorter events, 25.9 us)
Async XLA Ops:
  1.4 9.0 %copy-start = (bf16[1,8,128,128]{3,2,1,0:T(8,128)(2,1)S(1)}, bf16[1,8,128,128]{3,2,1,0:T(8,128)(2,1)}, u32[]{:S(2)}) copy-start(bf16[1,8,128,128]{3,2,1,0:T(8,128)(2,1)} %param.4) | copy-start | bytes 786436
  1.5 12.9 %collective-permute-start.2 = (f32[2,128,128]{2,0,1:T(2,128)S(1)}, f32[2,128,128]{2,0,1:T(2,128)S(1)}, u32[]{:S(2)}, u32[]{:S(2)}) collective-permute-start(f32[2,128,128]{2,0,1:T(2,128)S(1)} %get-tuple-element.39), channel_id=1, source_target_pairs={{0,1},{1,2},{2,3},{3,0},{4,5},{5,6},{6,7},{7,4},{8,9},{9,10},{10,1... | collective-permute-start | bytes 393224 | tf_op jit(solution)/shard_map/ppermute | solution.py:24
  5.7 6.7 %copy-start.24 = (s32[2,1,1]{0,2,1:T(1,128)S(1)}, s32[2,1,1]{0,2,1:T(1,128)}, u32[]{:S(2)}) copy-start(s32[2,1,1]{0,2,1:T(1,128)} %param.7) | copy-start | bytes 28
  5.8 8.9 %collective-permute-start.3 = (f32[2,128,128]{2,0,1:T(2,128)S(1)}, f32[2,128,128]{2,0,1:T(2,128)S(1)}, u32[]{:S(2)}, u32[]{:S(2)}) collective-permute-start(f32[2,128,128]{2,0,1:T(2,128)S(1)} %get-tuple-element.40), channel_id=1, source_target_pairs={{1,0},{2,1},{3,2},{0,3},{5,4},{6,5},{7,6},{4,7},{9,8},{10,9},{11,1... | collective-permute-start | bytes 393224 | tf_op jit(solution)/shard_map/ppermute | solution.py:25
  10.5 17.5 %collective-permute-start.1 = (bf16[1,8,128,128]{3,1,2,0:T(8,128)(2,1)S(1)}, bf16[1,8,128,128]{3,1,2,0:T(8,128)(2,1)S(1)}, u32[]{:S(2)}, u32[]{:S(2)}) collective-permute-start(bf16[1,8,128,128]{3,1,2,0:T(8,128)(2,1)S(1)} %copy.38), channel_id=1, source_target_pairs={{0,4},{4,8},{8,12},{12,16},{16,20},{20,24},{24,28},{28,32},{32,36}... | collective-permute-start | bytes 786440 | tf_op jit(solution)/shard_map/ppermute | solution.py:32
  28.0 32.9 %copy-start.4 = (bf16[1,8,128,128]{3,1,2,0:T(8,128)(2,1)}, bf16[1,8,128,128]{3,1,2,0:T(8,128)(2,1)S(1)}, u32[]{:S(2)}) copy-start(bf16[1,8,128,128]{3,1,2,0:T(8,128)(2,1)S(1)} %collective-permute-done.1) | copy-start | bytes 786436
  28.0 18.1 %collective-permute-start.9 = (bf16[1,8,128,128]{3,1,2,0:T(8,128)(2,1)S(1)}, bf16[1,8,128,128]{3,1,2,0:T(8,128)(2,1)S(1)}, u32[]{:S(2)}, u32[]{:S(2)}) collective-permute-start(bf16[1,8,128,128]{3,1,2,0:T(8,128)(2,1)S(1)} %collective-permute-done.1), channel_id=1, source_target_pairs={{0,4},{4,8},{8,12},{12,16},{16,20},{20,24},{24,28},{28,32},{32,36}... | collective-permute-start | bytes 786440 | tf_op jit(solution)/shard_map/ppermute | solution.py:32
  46.0 14.8 %copy-start.1 = (bf16[1,8,128,128]{3,1,2,0:T(8,128)(2,1)}, bf16[1,8,128,128]{3,1,2,0:T(8,128)(2,1)S(1)}, u32[]{:S(2)}) copy-start(bf16[1,8,128,128]{3,1,2,0:T(8,128)(2,1)S(1)} %collective-permute-done.9) | copy-start | bytes 786436
  46.5 2.9 %copy-start.9 = (f32[8,128,127]{2,0,1:T(8,128)}, f32[8,128,127]{2,0,1:T(8,128)S(1)}, u32[]{:S(2)}) copy-start(f32[8,128,127]{2,0,1:T(8,128)S(1)} %slice_bitcast_fusion.1) | copy-start | bytes 1560580
  52.8 6.1 %copy-start.23 = (f32[1,1,1,128,128]{4,2,3,1,0:T(1,128)S(1)}, f32[1,1,1,128,128]{4,2,3,1,0:T(1,128)}, u32[]{:S(2)}) copy-start(f32[1,1,1,128,128]{4,2,3,1,0:T(1,128)} %get-tuple-element.35) | copy-start | bytes 196612
  53.6 10.0 %collective-permute-start.10 = (f32[1,1,1,128,128]{4,2,3,1,0:T(1,128)}, f32[1,1,1,128,128]{4,2,3,1,0:T(1,128)S(1)}, u32[]{:S(2)}, u32[]{:S(2)}) collective-permute-start(f32[1,1,1,128,128]{4,2,3,1,0:T(1,128)} %get-tuple-element.36), channel_id=1, source_target_pairs={{1,0},{2,1},{3,2},{0,3},{5,4},{6,5},{7,6},{4,7},{9,8},{10,9},{11,1... | collective-permute-start | bytes 196616 | tf_op jit(solution)/shard_map/ppermute | solution.py:25
  58.9 6.8 %collective-permute-start.11 = (f32[1,1,1,128,128]{4,2,3,1,0:T(1,128)S(1)}, f32[1,1,1,128,128]{4,2,3,1,0:T(1,128)S(1)}, u32[]{:S(2)}, u32[]{:S(2)}) collective-permute-start(f32[1,1,1,128,128]{4,2,3,1,0:T(1,128)S(1)} %copy-done.23), channel_id=1, source_target_pairs={{0,1},{1,2},{2,3},{3,0},{4,5},{5,6},{6,7},{7,4},{8,9},{9,10},{10,1... | collective-permute-start | bytes 196616 | tf_op jit(solution)/shard_map/ppermute | solution.py:24
  62.1 3.6 %copy-start.14 = (f32[11,128,128]{2,0,1:T(8,128)S(1)}, f32[11,128,128]{2,0,1:T(8,128)}, u32[]{:S(2)}) copy-start(f32[11,128,128]{2,0,1:T(8,128)} %get-tuple-element.23) | copy-start | bytes 2162692
  65.7 2.2 %copy-start.11 = (f32[8,128,1]{2,0,1:T(8,128)S(1)}, f32[8,128,1]{2,0,1:T(8,128)}, u32[]{:S(2)}) copy-start(f32[8,128,1]{2,0,1:T(8,128)} %copy.54) | copy-start | bytes 12292
  65.7 2.2 %copy-start.13 = (f32[8,127,128]{2,0,1:T(8,128)S(1)}, f32[8,127,128]{2,0,1:T(8,128)}, u32[]{:S(2)}) copy-start(f32[8,127,128]{2,0,1:T(8,128)} %slice_bitcast_fusion.5) | copy-start | bytes 1560580
  65.8 2.3 %copy-start.18 = (f32[8,128,127]{2,0,1:T(8,128)S(1)}, f32[8,128,127]{2,0,1:T(8,128)}, u32[]{:S(2)}) copy-start(f32[8,128,127]{2,0,1:T(8,128)} %slice_bitcast_fusion) | copy-start | bytes 1560580
  65.8 2.4 %copy-start.19 = (f32[8,128,1]{2,0,1:T(8,128)S(1)}, f32[8,128,1]{2,0,1:T(8,128)}, u32[]{:S(2)}) copy-start(f32[8,128,1]{2,0,1:T(8,128)} %copy.56) | copy-start | bytes 12292
  65.8 2.6 %copy-start.22 = (f32[8,127,128]{2,0,1:T(8,128)S(1)}, f32[8,127,128]{2,0,1:T(8,128)}, u32[]{:S(2)}) copy-start(f32[8,127,128]{2,0,1:T(8,128)} %slice_bitcast_fusion.4) | copy-start | bytes 1560580
  72.6 21.5 %collective-permute-start.4 = (f32[1,1,1,128,128]{4,3,2,1,0:T(8,128)}, f32[1,1,1,128,128]{4,3,2,1,0:T(8,128)S(1)}, u32[]{:S(2)}, u32[]{:S(2)}) collective-permute-start(f32[1,1,1,128,128]{4,3,2,1,0:T(8,128)} %bitcast.63), channel_id=1, source_target_pairs={{1,0},{2,1},{3,2},{0,3},{5,4},{6,5},{7,6},{4,7},{9,8},{10,9},{11,1... | collective-permute-start | bytes 196616 | tf_op jit(solution)/shard_map/ppermute | solution.py:25
  75.6 18.4 %collective-permute-start.5 = (f32[1,1,1,128,128]{4,3,2,1,0:T(8,128)}, f32[1,1,1,128,128]{4,3,2,1,0:T(8,128)S(1)}, u32[]{:S(2)}, u32[]{:S(2)}) collective-permute-start(f32[1,1,1,128,128]{4,3,2,1,0:T(8,128)} %bitcast.64), channel_id=1, source_target_pairs={{0,1},{1,2},{2,3},{3,0},{4,5},{5,6},{6,7},{7,4},{8,9},{9,10},{10,1... | collective-permute-start | bytes 196616 | tf_op jit(solution)/shard_map/ppermute | solution.py:24
  88.2 16.7 %collective-permute-start.12 = (f32[1,1,1,128,128]{4,3,2,1,0:T(8,128)}, f32[1,1,1,128,128]{4,3,2,1,0:T(8,128)S(1)}, u32[]{:S(2)}, u32[]{:S(2)}) collective-permute-start(f32[1,1,1,128,128]{4,3,2,1,0:T(8,128)} %bitcast.69), channel_id=1, source_target_pairs={{1,0},{2,1},{3,2},{0,3},{5,4},{6,5},{7,6},{4,7},{9,8},{10,9},{11,1... | collective-permute-start | bytes 196616 | tf_op jit(solution)/shard_map/ppermute | solution.py:25
  91.2 13.7 %collective-permute-start.13 = (f32[1,1,1,128,128]{4,3,2,1,0:T(8,128)}, f32[1,1,1,128,128]{4,3,2,1,0:T(8,128)S(1)}, u32[]{:S(2)}, u32[]{:S(2)}) collective-permute-start(f32[1,1,1,128,128]{4,3,2,1,0:T(8,128)} %bitcast.70), channel_id=1, source_target_pairs={{0,1},{1,2},{2,3},{3,0},{4,5},{5,6},{6,7},{7,4},{8,9},{9,10},{10,1... | collective-permute-start | bytes 196616 | tf_op jit(solution)/shard_map/ppermute | solution.py:24
  98.0 6.1 %copy-start.15 = (f32[1,1,8,128,127]{4,2,3,1,0:T(8,128)S(1)}, f32[1,1,8,128,127]{4,2,3,1,0:T(8,128)}, u32[]{:S(2)}) copy-start(f32[1,1,8,128,127]{4,2,3,1,0:T(8,128)} %slice.339) | copy-start | bytes 1560580
  98.0 6.1 %copy-start.21 = (f32[1,1,8,127,128]{4,2,3,1,0:T(8,128)S(1)}, f32[1,1,8,127,128]{4,2,3,1,0:T(8,128)}, u32[]{:S(2)}) copy-start(f32[1,1,8,127,128]{4,2,3,1,0:T(8,128)} %slice.335) | copy-start | bytes 1560580
  98.1 6.8 %collective-permute-start.6 = (f32[1,1,1,128,128]{4,3,2,1,0:T(8,128)S(1)}, f32[1,1,1,128,128]{4,3,2,1,0:T(8,128)S(1)}, u32[]{:S(2)}, u32[]{:S(2)}) collective-permute-start(f32[1,1,1,128,128]{4,3,2,1,0:T(8,128)S(1)} %bitcast.246), channel_id=1, source_target_pairs={{1,0},{2,1},{3,2},{0,3},{5,4},{6,5},{7,6},{4,7},{9,8},{10,9},{11,1... | collective-permute-start | bytes 196616 | tf_op jit(solution)/shard_map/ppermute | solution.py:25
  101.7 8.0 %collective-permute-start.7 = (f32[1,1,1,128,128]{4,3,2,1,0:T(8,128)S(1)}, f32[1,1,1,128,128]{4,3,2,1,0:T(8,128)S(1)}, u32[]{:S(2)}, u32[]{:S(2)}) collective-permute-start(f32[1,1,1,128,128]{4,3,2,1,0:T(8,128)S(1)} %bitcast.245), channel_id=1, source_target_pairs={{0,1},{1,2},{2,3},{3,0},{4,5},{5,6},{6,7},{7,4},{8,9},{9,10},{10,1... | collective-permute-start | bytes 196616 | tf_op jit(solution)/shard_map/ppermute | solution.py:24
  110.7 22.3 %collective-permute-start.14 = (f32[1,8,128,128]{3,1,2,0:T(8,128)S(1)}, f32[1,8,128,128]{3,1,2,0:T(8,128)S(1)}, u32[]{:S(2)}, u32[]{:S(2)}) collective-permute-start(f32[1,8,128,128]{3,1,2,0:T(8,128)S(1)} %get-tuple-element.15), channel_id=1, source_target_pairs={{0,4},{4,8},{8,12},{12,16},{16,20},{20,24},{24,28},{28,32},{32,36}... | collective-permute-start | bytes 1572872 | tf_op jit(solution)/shard_map/ppermute | solution.py:32
  113.3 19.7 %copy-start.3 = (bf16[1,8,128,128]{3,1,2,0:T(8,128)(2,1)S(1)}, bf16[1,8,128,128]{3,1,2,0:T(8,128)(2,1)}, u32[]{:S(2)}) copy-start(bf16[1,8,128,128]{3,1,2,0:T(8,128)(2,1)} %copy-done.1) | copy-start | bytes 786436
  113.4 19.7 %copy-start.20 = (f32[1,1,8,128,128]{4,2,3,1,0:T(8,128)S(1)}, f32[1,1,8,128,128]{4,2,3,1,0:T(8,128)}, u32[]{:S(2)}) copy-start(f32[1,1,8,128,128]{4,2,3,1,0:T(8,128)} %get-tuple-element.8) | copy-start | bytes 1572868
  133.7 30.7 %collective-permute-start.15 = (f32[1,8,128,128]{3,1,2,0:T(8,128)S(1)}, f32[1,8,128,128]{3,1,2,0:T(8,128)S(1)}, u32[]{:S(2)}, u32[]{:S(2)}) collective-permute-start(f32[1,8,128,128]{3,1,2,0:T(8,128)S(1)} %get-tuple-element.5), channel_id=1, source_target_pairs={{0,504},{4,508},{8,0},{12,4},{16,8},{20,12},{24,16},{28,20},{32,24... | collective-permute-start | bytes 1572872 | tf_op jit(solution)/shard_map/ppermute | solution.py:32
  135.6 13.0 %collective-permute-start = (bf16[1]{0:T(256)(128)(2,1)}, bf16[1]{0:T(256)(128)(2,1)}, u32[]{:S(2)}, u32[]{:S(2)}) collective-permute-start(bf16[1]{0:T(256)(128)(2,1)} %convert_element_type.21), channel_id=1, source_target_pairs={{0,4},{4,8},{8,12},{12,16},{16,20},{20,24},{24,28},{28,32},{32,36}... | collective-permute-start | bytes 14 | tf_op jit(solution)/shard_map/ppermute | solution.py:32
  149.9 13.2 %collective-permute-start.8 = (bf16[1]{0:T(256)(128)(2,1)}, bf16[1]{0:T(256)(128)(2,1)}, u32[]{:S(2)}, u32[]{:S(2)}) collective-permute-start(bf16[1]{0:T(256)(128)(2,1)} %collective-permute-done), channel_id=1, source_target_pairs={{0,4},{4,8},{8,12},{12,16},{16,20},{20,24},{24,28},{28,32},{32,36}... | collective-permute-start | bytes 14 | tf_op jit(solution)/shard_map/ppermute | solution.py:32
  (9 other events, 16.2 us)
where the time goes:
time: 166 us; the launch traced here: 165 us
  waiting for transfers between devices  73.5 us (44%)
  starting transfers between devices  46 us (28%)
  local copies, waits for them, and re-layouts  25.7 us (15%)
  other arithmetic  15.2 us (9%)
  between operations  5.12 us (3%)
    ppermute x6, waiting for transfers between devices, passed_along(): return lax.ppermute(x, axis, [(i, (i + by) % size) for i in range(size)])  66.4 us
    ppermute x5, starting transfers between devices, with_halo(): after = lax.ppermute(leading, axis, down)  19.5 us
    ppermute x5, starting transfers between devices, with_halo(): before = lax.ppermute(last, axis, up)  14.2 us
    ppermute x6, starting transfers between devices, passed_along(): return lax.ppermute(x, axis, [(i, (i + by) % size) for i in range(size)])  12.3 us
    ppermute x5, waiting for transfers between devices, with_halo(): before = lax.ppermute(last, axis, up)  6.81 us
    mul x3, other arithmetic, stencil_apply(): flux_x = coef_x * (jnp.roll(center, -1, 3) - center)  4.74 us
    mul x3, other arithmetic, stencil_apply(): flux_z = coef_z * (field[:, :, 1:] - field[:, :, :-1])  4.07 us
    concatenate x4, local copies, waits for them, and re-layouts, stencil_apply(): part_y = flux_y - jnp.roll(flux_y, 1, 4)  3.83 us
  transfers between devices with their start and end apart: 16, of which 8 were waited for; matrix products, arithmetic and copies ran while one was open for 13% of the time, Pallas kernels for 0%

commit v1 on v0

v1 whole, which is shorter than its diff:
```python
import math

import jax
import jax.numpy as jnp
from jax import lax
from jax.sharding import PartitionSpec as P

SWEEPS = 2


FOUR_PI = 4.0 * math.pi
KAPPA_SQ = 4.0
CHEB_CENTER = 28.0
CHEB_HALF = 24.0
HALO = SWEEPS


def shifted(x, axis, by):
    size = lax.axis_size(axis)
    return lax.ppermute(x, axis, [(i, (i + by) % size) for i in range(size)])


def z_halo(x, dim, width):
    length = x.shape[dim]
    last = lax.slice_in_dim(x, length - width, length, axis=dim)
    leading = lax.slice_in_dim(x, 0, width, axis=dim)
    before = shifted(last, "depth", 1)
    after = shifted(leading, "depth", -1)
    return jnp.concatenate([before, x, after], axis=dim)


def stencil(field, coef_z, coef_x, coef_y):
    flux_z = coef_z * (field[..., 1:, :, :] - field[..., :-1, :, :])
    part_z = flux_z[..., 1:, :, :] - flux_z[..., :-1, :, :]
    center = field[..., 1:-1, :, :]
    flux_x = coef_x * (jnp.roll(center, -1, -2) - center)
    part_x = flux_x - jnp.roll(flux_x, 1, -2)
    flux_y = coef_y * (jnp.roll(center, -1, -1) - center)
    part_y = flux_y - jnp.roll(flux_y, 1, -1)
    return KAPPA_SQ * center - (part_z + part_x + part_y)


def potential_of(source, face_z, face_x, face_y):
    sigma = CHEB_CENTER / CHEB_HALF
    factor = CHEB_HALF / CHEB_CENTER
    direction = source / CHEB_CENTER
    solution = direction
    remainder = source
    lo = 0
    for sweep in range(SWEEPS):
        n = direction.shape[-3]
        applied = stencil(
            direction,
            face_z[lo : lo + n - 1],
            face_x[lo + 1 : lo + n - 1],
            face_y[lo + 1 : lo + n - 1],
        )
        lo += 1
        remainder = remainder[..., 1:-1, :, :] - applied
        factor_next = 1.0 / (2.0 * sigma - factor)
        direction = factor_next * factor * direction[..., 1:-1, :, :] + 2.0 * factor_next / CHEB_HALF * remainder
        solution = solution[..., 1:-1, :, :] + direction
        factor = factor_next
    return solution


def on_device(orbitals, dielectric, occupied, plan):
    psi = orbitals[0]
    occ = occupied.astype(jnp.bfloat16)[0]
    flags = plan.astype(jnp.bfloat16).reshape(plan.shape[0])

    padded_diel = z_halo(dielectric, 0, HALO)
    face_z = (padded_diel[:-1] + padded_diel[1:]) * 0.5
    face_x = (padded_diel + jnp.roll(padded_diel, -1, 1)) * 0.5
    face_y = (padded_diel + jnp.roll(padded_diel, -1, 2)) * 0.5

    ticks = plan.shape[0]
    lower = psi * occ
    slabs = [psi]
    for tick in range(1, ticks + 1):
        slabs.append(shifted(lower, "band", tick))
    for tick in range(1, ticks + 1):
        slabs.append(shifted(psi * (flags[tick - 1] * occ), "band", -tick))
    stack = jnp.stack(slabs)
    wide = z_halo(stack, 1, HALO).astype(jnp.float32)
    own = wide[0]
    partners = wide[1:]
    density = (FOUR_PI * own)[None] * partners
    potential = potential_of(density, face_z, face_x, face_y)
    weights = jnp.concatenate(
        [plan.astype(jnp.float32).reshape(ticks), jnp.ones((ticks,), jnp.float32)]
    )
    terms = weights[:, None, None, None] * potential * partners[:, HALO:-HALO]
    totals = jnp.sum(terms, axis=0)
    return -totals[None]


def solution(mesh):
    placed = (
        P("band", "depth", None, None),
        P("depth", None, None),
        P("band"),
        P(None, "band", None),
    )
    return jax.shard_map(
        on_device,
        mesh=mesh,
        in_specs=placed,
        out_specs=P("band", "depth", None, None),
        check_vma=False,
    )
```

time: 166 us -> 97.5 us (0.59)
  the two profiles are of different devices: /device:TPU:64 before, /device:TPU:56 now
where the time goes in v1:
time: 97.5 us; the launch traced here: 95.8 us
  starting transfers between devices  32.6 us (33%)
  waiting for transfers between devices  27.7 us (28%)
  other arithmetic  17.8 us (18%)
  local copies, waits for them, and re-layouts  15.4 us (16%)
  between operations  2.31 us (2%)
    ppermute x8, starting transfers between devices, shifted(): return lax.ppermute(x, axis, [(i, (i + by) % size) for i in range(size)])  32.6 us
    ppermute x8, waiting for transfers between devices, shifted(): return lax.ppermute(x, axis, [(i, (i + by) % size) for i in range(size)])  27.7 us
    add x1, other arithmetic, potential_of(): factor_next * factor * direction[..., 1:-1, :, :]  4.34 us
    mul x1, other arithmetic, stencil(): flux_x = coef_x * (jnp.roll(center, -1, -2) - center)  4.12 us
    slice x4, local copies, waits for them, and re-layouts, stencil(): flux_y = coef_y * (jnp.roll(center, -1, -1) - center)  3.21 us
    reduce_sum x1, other arithmetic, on_device(): totals = jnp.sum(terms, axis=0)  3.1 us
    unnamed x17, local copies, waits for them, and re-layouts  2.25 us
    slice x4, local copies, waits for them, and re-layouts, stencil(): flux_x = coef_x * (jnp.roll(center, -1, -2) - center)  2.19 us
  transfers between devices with their start and end apart: 8, of which 3 were waited for; matrix products, arithmetic and copies ran while one was open for 7% of the time, Pallas kernels for 0%

profile of v1, /device:TPU:56, one launch (start us, length us, event | category | flops | bytes accessed | tf_op | source)
XLA Modules:
  0.0 95.8 jit_solution(4208703855741736276)
XLA Ops:
  0.0 1.0 %fusion.25 = (f32[2,128,128]{2,1,0:T(8,128)S(1)}, f32[2,128,128]{2,1,0:T(8,128)S(1)}) fusion(f32[8,128,128]{2,1,0:T(8,128)} %param.5), kind=kLoop, calls=%fused_computation.59 | loop fusion | bytes 524288 | tf_op jit(solution)/shard_map/slice | solution.py:26
  1.1 4.3 %collective-permute-start.6 = (f32[2,128,128]{2,1,0:T(8,128)S(1)}, f32[2,128,128]{2,1,0:T(8,128)S(1)}, u32[]{:S(2)}, u32[]{:S(2)}) collective-permute-start(f32[2,128,128]{2,1,0:T(8,128)S(1)} %get-tuple-element.19), channel_id=1, source_target_pairs={{0,1},{1,2},{2,3},{3,0},{4,5},{5,6},{6,7},{7,4},{8,9},{9,10},{10,1... | collective-permute-start | bytes 393224 | tf_op jit(solution)/shard_map/ppermute | solution.py:20
  6.0 0.7 convert_bitcast_fusion
  8.6 1.2 %multiply_bitcast_fusion = (bf16[8,128,128]{2,1,0:T(8,128)(2,1)S(1)}, bf16[8,128,128]{2,1,0:T(8,128)(2,1)S(1)}, bf16[8,128,128]{2,1,0:T(8,128)(2,1)S(1)}, bf16[5,8,128,128]{3,2,1,0:T(8,128)(2,1)S(1)}) fusion(bf16[1,8,128,128]{3,2,1,0:T(8,128)(2,1)} %param.4, bf16[]{:T(256)S(6)} %mul.165, bf16[]{:T(256)S(6)} %mul.161, bf16[]{:T(256)} %bitcast.1), kind=kLoop, calls=%fused_computation.50 | loop fusion | flops 1310719 | bytes 1310726 | tf_op jit(solution)/shard_map/mul | solution.py:83
  9.8 9.2 %collective-permute-start.1 = (bf16[8,128,128]{2,1,0:T(8,128)(2,1)S(1)}, bf16[8,128,128]{2,1,0:T(8,128)(2,1)S(1)}, u32[]{:S(2)}, u32[]{:S(2)}) collective-permute-start(bf16[8,128,128]{2,1,0:T(8,128)(2,1)S(1)} %get-tuple-element.22), channel_id=1, source_target_pairs={{0,8},{4,12},{8,16},{12,20},{16,24},{20,28},{24,32},{28,36},{32,40... | collective-permute-start | bytes 786440 | tf_op jit(solution)/shard_map/ppermute | solution.py:20
  19.1 1.9 %collective-permute-start = (bf16[8,128,128]{2,1,0:T(8,128)(2,1)S(1)}, bf16[8,128,128]{2,1,0:T(8,128)(2,1)S(1)}, u32[]{:S(2)}, u32[]{:S(2)}) collective-permute-start(bf16[8,128,128]{2,1,0:T(8,128)(2,1)S(1)} %get-tuple-element.22), channel_id=1, source_target_pairs={{0,4},{4,8},{8,12},{12,16},{16,20},{20,24},{24,28},{28,32},{32,36}... | collective-permute-start | bytes 786440 | tf_op jit(solution)/shard_map/ppermute | solution.py:20
  21.0 4.3 %collective-permute-start.7 = (f32[2,128,128]{2,1,0:T(8,128)S(1)}, f32[2,128,128]{2,1,0:T(8,128)S(1)}, u32[]{:S(2)}, u32[]{:S(2)}) collective-permute-start(f32[2,128,128]{2,1,0:T(8,128)S(1)} %get-tuple-element.18), channel_id=1, source_target_pairs={{0,3},{1,0},{2,1},{3,2},{4,7},{5,4},{6,5},{7,6},{8,11},{9,8},{10,9... | collective-permute-start | bytes 393224 | tf_op jit(solution)/shard_map/ppermute | solution.py:20
  25.3 1.9 %collective-permute-start.3 = (bf16[8,128,128]{2,1,0:T(8,128)(2,1)S(1)}, bf16[8,128,128]{2,1,0:T(8,128)(2,1)S(1)}, u32[]{:S(2)}, u32[]{:S(2)}) collective-permute-start(bf16[8,128,128]{2,1,0:T(8,128)(2,1)S(1)} %get-tuple-element.20), channel_id=1, source_target_pairs={{0,504},{4,508},{8,0},{12,4},{16,8},{20,12},{24,16},{28,20},{32,24... | collective-permute-start | bytes 786440 | tf_op jit(solution)/shard_map/ppermute | solution.py:20
  27.2 3.4 %collective-permute-start.2 = (bf16[8,128,128]{2,1,0:T(8,128)(2,1)S(1)}, bf16[8,128,128]{2,1,0:T(8,128)(2,1)S(1)}, u32[]{:S(2)}, u32[]{:S(2)}) collective-permute-start(bf16[8,128,128]{2,1,0:T(8,128)(2,1)S(1)} %get-tuple-element.21), channel_id=1, source_target_pairs={{0,508},{4,0},{8,4},{12,8},{16,12},{20,16},{24,20},{28,24},{32,28}... | collective-permute-start | bytes 786440 | tf_op jit(solution)/shard_map/ppermute | solution.py:20
  31.2 5.5 %collective-permute-done.2 = bf16[8,128,128]{2,1,0:T(8,128)(2,1)S(1)} collective-permute-done((bf16[8,128,128]{2,1,0:T(8,128)(2,1)S(1)}, bf16[8,128,128]{2,1,0:T(8,128)(2,1)S(1)}, u32[]{:S(2)}, u32[]{:S(2)}) %collective-permute-start.2) | collective-permute-done | bytes 262176 | tf_op jit(solution)/shard_map/ppermute | solution.py:20
  36.7 12.3 %collective-permute-done.3 = bf16[8,128,128]{2,1,0:T(8,128)(2,1)S(1)} collective-permute-done((bf16[8,128,128]{2,1,0:T(8,128)(2,1)S(1)}, bf16[8,128,128]{2,1,0:T(8,128)(2,1)S(1)}, u32[]{:S(2)}, u32[]{:S(2)}) %collective-permute-start.3) | collective-permute-done | bytes 262176 | tf_op jit(solution)/shard_map/ppermute | solution.py:20
  49.1 1.9 %collective-permute-start.4 = (bf16[5,2,128,128]{3,2,1,0:T(8,128)(2,1)S(1)}, bf16[5,2,128,128]{3,2,1,0:T(8,128)(2,1)S(1)}, u32[]{:S(2)}, u32[]{:S(2)}) collective-permute-start(bf16[5,2,128,128]{3,2,1,0:T(8,128)(2,1)S(1)} %get-tuple-element.14), channel_id=1, source_target_pairs={{0,1},{1,2},{2,3},{3,0},{4,5},{5,6},{6,7},{7,4},{8,9},{9,10},{10,1... | collective-permute-start | bytes 983048 | tf_op jit(solution)/shard_map/ppermute | solution.py:20
  51.1 5.7 %collective-permute-start.5 = (bf16[5,2,128,128]{3,2,1,0:T(8,128)(2,1)S(1)}, bf16[5,2,128,128]{3,2,1,0:T(8,128)(2,1)S(1)}, u32[]{:S(2)}, u32[]{:S(2)}) collective-permute-start(bf16[5,2,128,128]{3,2,1,0:T(8,128)(2,1)S(1)} %get-tuple-element.15), channel_id=1, source_target_pairs={{0,3},{1,0},{2,1},{3,2},{4,7},{5,4},{6,5},{7,6},{8,11},{9,8},{10,9... | collective-permute-start | bytes 983048 | tf_op jit(solution)/shard_map/ppermute | solution.py:20
  57.1 0.8 slice.264
  57.9 0.9 slice.243
  58.8 0.8 slice.269
  59.6 0.9 slice.250
  60.6 9.8 %collective-permute-done.5 = bf16[5,2,128,128]{3,2,1,0:T(8,128)(2,1)S(1)} collective-permute-done((bf16[5,2,128,128]{3,2,1,0:T(8,128)(2,1)S(1)}, bf16[5,2,128,128]{3,2,1,0:T(8,128)(2,1)S(1)}, u32[]{:S(2)}, u32[]{:S(2)}) %collective-permute-start.5) | collective-permute-done | bytes 327712 | tf_op jit(solution)/shard_map/ppermute | solution.py:20
  70.8 1.0 broadcast_multiply_fusion
  72.3 0.7 slice.251
  73.1 1.9 %slice.244 = f32[4,10,127,128]{3,2,1,0:T(8,128)} slice(f32[4,12,128,128]{3,2,1,0:T(8,128)S(1)} %get-tuple-element.7), slice={[0:4], [1:11], [1:128], [0:128]} | slice | bytes 5201920 | tf_op jit(solution)/shard_map/jit(_roll_static)/slice | solution.py:36
  75.0 1.7 %slice.252 = f32[4,10,128,1]{3,2,1,0:T(8,128)} slice(f32[4,12,128,128]{3,2,1,0:T(8,128)S(1)} %get-tuple-element.7), slice={[0:4], [1:11], [0:128], [0:1]} | slice | bytes 40960 | tf_op jit(solution)/shard_map/jit(_roll_static)/slice | solution.py:38
  76.7 4.1 %fusion.5 = (f32[4,10,128,128]{3,2,1,0:T(8,128)S(1)}, f32[4,10,128,128]{3,2,1,0:T(8,128)S(1)}) fusion(f32[4,10,1,128]{3,2,1,0:T(1,128)S(1)} %slice.245, f32[4,10,127,128]{3,2,1,0:T(8,128)} %slice.244, f32[10,128,128]{2,1,0:T(8,128)} %slice.243, f32[4,12,128,128]{3,2,1,0:T(8,128)S(1)} %get-tuple-element.7, f32[4,10,128,1]{3,2,1,0:T(8,128)} %slice.252, ...), kind=kLoop, calls=%fused_computation.9 | loop fusion | flops 3932160 | bytes 14417920 | tf_op jit(solution)/shard_map/mul | solution.py:36
  80.8 0.7 slice.253
  81.6 4.3 %multiply_add_fusion = (f32[4,10,128,128]{3,2,1,0:T(8,128)S(1)}, f32[4,10,128,128]{3,2,1,0:T(8,128)}, f32[4,10,128,128]{3,2,1,0:T(8,128)}) fusion(f32[4,12,128,128]{3,2,1,0:T(8,128)S(1)} %get-tuple-element.7, f32[4,10,128,128]{3,2,1,0:T(8,128)S(1)} %get-tuple-element.11, f32[4,10,128,127]{3,2,1,0:T(8,128)S(1)} %bitcast.28, f32[4,10,128,1]{3,2,1,0:T(8,128)S(1)} %slice.253, ...), kind=kLoop, calls=%fused_computation.14 | loop fusion | flops 8519680 | bytes 28835840 | tf_op jit(solution)/shard_map/add | solution.py:61
  86.2 0.6 slice.270
  87.0 0.9 slice-done
  88.3 0.6 copy-done.3
  89.1 0.9 fusion.18
  90.8 1.1 %copy-done = f32[4,10,128,128]{3,2,1,0:T(8,128)S(1)} copy-done((f32[4,10,128,128]{3,2,1,0:T(8,128)S(1)}, f32[4,10,128,128]{3,2,1,0:T(8,128)}, u32[]{:S(2)}) %copy-start) | copy-done | bytes 2621464
  91.9 3.1 %fusion.8 = f32[8,128,128]{2,1,0:T(8,128)S(1)} fusion(f32[5,12,128,128]{3,2,1,0:T(8,128)S(1)} %maximum_convert_fusion, f32[4,9,128,128]{3,2,1,0:T(8,128)S(1)} %fusion.7, f32[4,10,128,128]{3,2,1,0:T(8,128)S(1)} %copy-done, f32[4,10,128,128]{3,2,1,0:T(8,128)S(1)} %copy-done.1, f32[4,8,128,128]{3,2,1,0:T(8,128)S(1)} %get-tuple-element.13, ...), kind=kLoop, calls=%fused_computation.18 | loop fusion | flops 9306112 | bytes 21495824 | tf_op jit(solution)/shard_map/reduce_sum | solution.py:94
  95.0 0.8 negate_bitcast_fusion
  (42 shorter events, 4.3 us)
Async XLA Ops:
  0.0 30.6 %copy-start.5 = (f32[8,128,128]{2,1,0:T(8,128)S(1)}, f32[8,128,128]{2,1,0:T(8,128)}, u32[]{:S(2)}) copy-start(f32[8,128,128]{2,1,0:T(8,128)} %param.5) | copy-start | bytes 1572868
  1.1 26.2 %collective-permute-start.6 = (f32[2,128,128]{2,1,0:T(8,128)S(1)}, f32[2,128,128]{2,1,0:T(8,128)S(1)}, u32[]{:S(2)}, u32[]{:S(2)}) collective-permute-start(f32[2,128,128]{2,1,0:T(8,128)S(1)} %get-tuple-element.19), channel_id=1, source_target_pairs={{0,1},{1,2},{2,3},{3,0},{4,5},{5,6},{6,7},{7,4},{8,9},{9,10},{10,1... | collective-permute-start | bytes 393224 | tf_op jit(solution)/shard_map/ppermute | solution.py:20
  9.8 21.3 %collective-permute-start.1 = (bf16[8,128,128]{2,1,0:T(8,128)(2,1)S(1)}, bf16[8,128,128]{2,1,0:T(8,128)(2,1)S(1)}, u32[]{:S(2)}, u32[]{:S(2)}) collective-permute-start(bf16[8,128,128]{2,1,0:T(8,128)(2,1)S(1)} %get-tuple-element.22), channel_id=1, source_target_pairs={{0,8},{4,12},{8,16},{12,20},{16,24},{20,28},{24,32},{28,36},{32,40... | collective-permute-start | bytes 786440 | tf_op jit(solution)/shard_map/ppermute | solution.py:20
  19.1 12.0 %collective-permute-start = (bf16[8,128,128]{2,1,0:T(8,128)(2,1)S(1)}, bf16[8,128,128]{2,1,0:T(8,128)(2,1)S(1)}, u32[]{:S(2)}, u32[]{:S(2)}) collective-permute-start(bf16[8,128,128]{2,1,0:T(8,128)(2,1)S(1)} %get-tuple-element.22), channel_id=1, source_target_pairs={{0,4},{4,8},{8,12},{12,16},{16,20},{20,24},{24,28},{28,32},{32,36}... | collective-permute-start | bytes 786440 | tf_op jit(solution)/shard_map/ppermute | solution.py:20
  21.0 9.7 %collective-permute-start.7 = (f32[2,128,128]{2,1,0:T(8,128)S(1)}, f32[2,128,128]{2,1,0:T(8,128)S(1)}, u32[]{:S(2)}, u32[]{:S(2)}) collective-permute-start(f32[2,128,128]{2,1,0:T(8,128)S(1)} %get-tuple-element.18), channel_id=1, source_target_pairs={{0,3},{1,0},{2,1},{3,2},{4,7},{5,4},{6,5},{7,6},{8,11},{9,8},{10,9... | collective-permute-start | bytes 393224 | tf_op jit(solution)/shard_map/ppermute | solution.py:20
  25.3 23.8 %collective-permute-start.3 = (bf16[8,128,128]{2,1,0:T(8,128)(2,1)S(1)}, bf16[8,128,128]{2,1,0:T(8,128)(2,1)S(1)}, u32[]{:S(2)}, u32[]{:S(2)}) collective-permute-start(bf16[8,128,128]{2,1,0:T(8,128)(2,1)S(1)} %get-tuple-element.20), channel_id=1, source_target_pairs={{0,504},{4,508},{8,0},{12,4},{16,8},{20,12},{24,16},{28,20},{32,24... | collective-permute-start | bytes 786440 | tf_op jit(solution)/shard_map/ppermute | solution.py:20
  27.2 9.5 %collective-permute-start.2 = (bf16[8,128,128]{2,1,0:T(8,128)(2,1)S(1)}, bf16[8,128,128]{2,1,0:T(8,128)(2,1)S(1)}, u32[]{:S(2)}, u32[]{:S(2)}) collective-permute-start(bf16[8,128,128]{2,1,0:T(8,128)(2,1)S(1)} %get-tuple-element.21), channel_id=1, source_target_pairs={{0,508},{4,0},{8,4},{12,8},{16,12},{20,16},{24,20},{28,24},{32,28}... | collective-permute-start | bytes 786440 | tf_op jit(solution)/shard_map/ppermute | solution.py:20
  49.1 11.5 %collective-permute-start.4 = (bf16[5,2,128,128]{3,2,1,0:T(8,128)(2,1)S(1)}, bf16[5,2,128,128]{3,2,1,0:T(8,128)(2,1)S(1)}, u32[]{:S(2)}, u32[]{:S(2)}) collective-permute-start(bf16[5,2,128,128]{3,2,1,0:T(8,128)(2,1)S(1)} %get-tuple-element.14), channel_id=1, source_target_pairs={{0,1},{1,2},{2,3},{3,0},{4,5},{5,6},{6,7},{7,4},{8,9},{9,10},{10,1... | collective-permute-start | bytes 983048 | tf_op jit(solution)/shard_map/ppermute | solution.py:20
  51.1 19.4 %collective-permute-start.5 = (bf16[5,2,128,128]{3,2,1,0:T(8,128)(2,1)S(1)}, bf16[5,2,128,128]{3,2,1,0:T(8,128)(2,1)S(1)}, u32[]{:S(2)}, u32[]{:S(2)}) collective-permute-start(bf16[5,2,128,128]{3,2,1,0:T(8,128)(2,1)S(1)} %get-tuple-element.15), channel_id=1, source_target_pairs={{0,3},{1,0},{2,1},{3,2},{4,7},{5,4},{6,5},{7,6},{8,11},{9,8},{10,9... | collective-permute-start | bytes 983048 | tf_op jit(solution)/shard_map/ppermute | solution.py:20
  60.6 11.2 %copy-start.2 = (f32[11,128,128]{2,1,0:T(8,128)}, f32[11,128,128]{2,1,0:T(8,128)S(1)}, u32[]{:S(2)}) copy-start(f32[11,128,128]{2,1,0:T(8,128)S(1)} %fusion.22) | copy-start | bytes 2162692
  86.8 1.1 %slice-start = ((f32[11,128,128]{2,1,0:T(8,128)}), f32[9,128,128]{2,1,0:T(8,128)S(1)}, s32[]{:S(2)}) async-start(f32[11,128,128]{2,1,0:T(8,128)} %copy-done.2), calls=%async_computation | async-start | bytes 1179648 | tf_op jit(solution)/shard_map/slice | solution.py:54
  87.9 1.0 %copy-start.3 = (f32[8,128,128]{2,1,0:T(8,128)S(1)}, f32[8,128,128]{2,1,0:T(8,128)}, u32[]{:S(2)}) copy-start(f32[8,128,128]{2,1,0:T(8,128)} %slice.264) | copy-start | bytes 1572868
  87.9 1.2 %copy-start.4 = (f32[8,128,128]{2,1,0:T(8,128)S(1)}, f32[8,128,128]{2,1,0:T(8,128)}, u32[]{:S(2)}) copy-start(f32[8,128,128]{2,1,0:T(8,128)} %slice.269) | copy-start | bytes 1572868
  89.1 1.7 %copy-start.1 = (f32[4,10,128,128]{3,2,1,0:T(8,128)S(1)}, f32[4,10,128,128]{3,2,1,0:T(8,128)}, u32[]{:S(2)}) copy-start(f32[4,10,128,128]{3,2,1,0:T(8,128)} %get-tuple-element.9) | copy-start | bytes 7864324
  90.0 1.9 %copy-start = (f32[4,10,128,128]{3,2,1,0:T(8,128)S(1)}, f32[4,10,128,128]{3,2,1,0:T(8,128)}, u32[]{:S(2)}) copy-start(f32[4,10,128,128]{3,2,1,0:T(8,128)} %get-tuple-element.6) | copy-start | bytes 7864324

commit v2 on v1

v2 whole, which is shorter than its diff:
```python
import math

import jax
import jax.numpy as jnp
from jax import lax
from jax.experimental import pallas as pl
from jax.experimental.pallas import tpu as pltpu
from jax.sharding import PartitionSpec as P

SWEEPS = 2


FOUR_PI = 4.0 * math.pi
KAPPA_SQ = 4.0
CHEB_CENTER = 28.0
CHEB_HALF = 24.0
HALO = SWEEPS


def shifted(x, axis, by):
    size = lax.axis_size(axis)
    return lax.ppermute(x, axis, [(i, (i + by) % size) for i in range(size)])


def z_halo(x, dim, width):
    length = x.shape[dim]
    last = lax.slice_in_dim(x, length - width, length, axis=dim)
    leading = lax.slice_in_dim(x, 0, width, axis=dim)
    before = shifted(last, "depth", 1)
    after = shifted(leading, "depth", -1)
    return jnp.concatenate([before, x, after], axis=dim)


def solve_kernel(weight_ref, psi_ref, eps_ref, out_ref, face_z, face_x, face_y, dens, first, rem, second, partial):
    layers, rows, cols = eps_ref.shape
    pairs = psi_ref.shape[0] - 1

    def faces(e, carry):
        cur = eps_ref[e]
        face_x[e] = (cur + pltpu.roll(cur, rows - 1, 0)) * 0.5
        face_y[e] = (cur + pltpu.roll(cur, cols - 1, 1)) * 0.5
        return carry

    lax.fori_loop(0, layers, faces, 0)

    def faces_z(e, carry):
        face_z[e] = (eps_ref[e] + eps_ref[e + 1]) * 0.5
        return carry

    lax.fori_loop(0, layers - 1, faces_z, 0)

    def applied(field, e):
        center = field[e]
        flux_up = face_z[e] * (field[e + 1] - center)
        flux_down = face_z[e - 1] * (center - field[e - 1])
        part_z = flux_up - flux_down
        flux_x = face_x[e] * (pltpu.roll(center, rows - 1, 0) - center)
        part_x = flux_x - pltpu.roll(flux_x, 1, 0)
        flux_y = face_y[e] * (pltpu.roll(center, cols - 1, 1) - center)
        part_y = flux_y - pltpu.roll(flux_y, 1, 1)
        return KAPPA_SQ * center - (part_z + part_x + part_y)

    sigma = CHEB_CENTER / CHEB_HALF
    factor = CHEB_HALF / CHEB_CENTER
    factor_one = 1.0 / (2.0 * sigma - factor)
    factor_two = 1.0 / (2.0 * sigma - factor_one)
    keep_one, mix_one = factor_one * factor, 2.0 * factor_one / CHEB_HALF
    keep_two, mix_two = factor_two * factor_one, 2.0 * factor_two / CHEB_HALF

    out_ref[...] = jnp.zeros(out_ref.shape, out_ref.dtype)
    for k in range(pairs):
        weight = weight_ref[k]

        def density(e, carry):
            own = psi_ref[0, e].astype(jnp.float32)
            partner = psi_ref[k + 1, e].astype(jnp.float32)
            value = (FOUR_PI * own) * partner
            dens[e] = value
            first[e] = value / CHEB_CENTER
            return carry

        lax.fori_loop(0, layers, density, 0)

        def sweep_one(e, carry):
            center = first[e]
            remainder = dens[e] - applied(first, e)
            direction = keep_one * center + mix_one * remainder
            rem[e] = remainder
            second[e] = direction
            partial[e] = center + direction
            return carry

        lax.fori_loop(1, layers - 1, sweep_one, 0)

        def sweep_two(e, carry):
            remainder = rem[e] - applied(second, e)
            direction = keep_two * second[e] + mix_two * remainder
            potential = partial[e] + direction
            partner = psi_ref[k + 1, e].astype(jnp.float32)
            out_ref[e - HALO] += (weight * potential) * partner
            return carry

        lax.fori_loop(HALO, layers - HALO, sweep_two, 0)
    out_ref[...] = -out_ref[...]


def solve(weights, wide, padded_diel):
    layers, rows, cols = padded_diel.shape
    pairs = wide.shape[0] - 1
    full = jax.ShapeDtypeStruct((layers, rows, cols), jnp.float32)
    vmem = pltpu.VMEM
    return pl.pallas_call(
        solve_kernel,
        out_shape=jax.ShapeDtypeStruct((layers - 2 * HALO, rows, cols), jnp.float32),
        in_specs=[
            pl.BlockSpec(memory_space=pltpu.SMEM),
            pl.BlockSpec(memory_space=vmem),
            pl.BlockSpec(memory_space=vmem),
        ],
        out_specs=pl.BlockSpec(memory_space=vmem),
        scratch_shapes=[vmem((layers - 1, rows, cols), jnp.float32)] + [vmem(full.shape, jnp.float32)] * 7,
        compiler_params=pltpu.CompilerParams(vmem_limit_bytes=48 * 1024 * 1024),
        cost_estimate=pl.CostEstimate(
            flops=pairs * 3 * layers * rows * cols * 30,
            transcendentals=0,
            bytes_accessed=wide.size * 2 + padded_diel.size * 4 + (layers - 2 * HALO) * rows * cols * 4,
        ),
    )(weights, wide, padded_diel)


def on_device(orbitals, dielectric, occupied, plan):
    psi = orbitals[0]
    occ = occupied.astype(jnp.bfloat16)[0]
    flags = plan.astype(jnp.bfloat16).reshape(plan.shape[0])
    padded_diel = z_halo(dielectric, 0, HALO)

    ticks = plan.shape[0]
    lower = psi * occ
    slabs = [psi]
    for tick in range(1, ticks + 1):
        slabs.append(shifted(lower, "band", tick))
    for tick in range(1, ticks + 1):
        slabs.append(shifted(psi * (flags[tick - 1] * occ), "band", -tick))
    wide = z_halo(jnp.stack(slabs), 1, HALO)
    weights = jnp.concatenate(
        [plan.astype(jnp.float32).reshape(ticks), jnp.ones((ticks,), jnp.float32)]
    )
    return solve(weights, wide, padded_diel)[None]


def solution(mesh):
    placed = (
        P("band", "depth", None, None),
        P("depth", None, None),
        P("band"),
        P(None, "band", None),
    )
    return jax.shard_map(
        on_device,
        mesh=mesh,
        in_specs=placed,
        out_specs=P("band", "depth", None, None),
        check_vma=False,
    )
```

time: 97.5 us -> 86.1 us (0.88); the launches traced: 95.8 us -> 85.8 us
  other arithmetic: 17.8 us -> 2.25 us
  Pallas kernels: 0 us -> 15.4 us
  local copies, waits for them, and re-layouts: 15.4 us -> 0.81 us
  waiting for transfers between devices: 27.7 us -> 34.5 us
  starting transfers between devices: 32.6 us -> 30.7 us
    pallas_call x0 -> x1, Pallas kernels: none -> 15.4 us  [solve(): pl.pallas_call(solve_kernel, out_shape=jax.ShapeDtypeStruct((layers - 2 *...]
    slice x22 -> x0, local copies, waits for them, and re-layouts: 12.5 us -> none  [the longest x4 3.21 us: stencil(): flux_y = coef_y * (jnp.roll(center, -1, -1) - center)]
    ppermute x8, waiting for transfers between devices: 27.7 us -> 34.5 us  [shifted(): return lax.ppermute(x, axis, [(i, (i + by) % size) for i in range(size)])]
    mul x7 -> x0, other arithmetic: 6.31 us -> none  [the longest x1 4.12 us: stencil(): flux_x = coef_x * (jnp.roll(center, -1, -2) - center)]
    add x1 -> x0, other arithmetic: 4.34 us -> none  [potential_of(): factor_next * factor * direction[..., 1:-1, :, :]]
    reduce_sum x1 -> x0, other arithmetic: 3.1 us -> none  [on_device(): totals = jnp.sum(terms, axis=0)]
    unnamed x17 -> x5, local copies, waits for them, and re-layouts: 2.25 us -> 0.12 us
    ppermute x8, starting transfers between devices: 32.6 us -> 30.7 us  [shifted(): return lax.ppermute(x, axis, [(i, (i + by) % size) for i in range(size)])]
  transfers between devices with their start and end apart: 8 -> 8, of which waited for: 3 -> 4; matrix products, arithmetic and copies ran while one was open for 7% -> 0% of each run, Pallas kernels for 0% -> 0%
where the time goes in v2:
time: 86.1 us; the launch traced here: 85.8 us
  waiting for transfers between devices  34.5 us (40%)
  starting transfers between devices  30.7 us (36%)
  Pallas kernels  15.4 us (18%)
  other arithmetic  2.25 us (3%)
  between operations  2.06 us (2%)
    ppermute x8, waiting for transfers between devices, shifted(): return lax.ppermute(x, axis, [(i, (i + by) % size) for i in range(size)])  34.5 us
    ppermute x8, starting transfers between devices, shifted(): return lax.ppermute(x, axis, [(i, (i + by) % size) for i in range(size)])  30.7 us
    pallas_call x1, Pallas kernels, solve(): pl.pallas_call(solve_kernel, out_shape=jax.ShapeDtypeStruct((layers - 2 *...  15.4 us
  transfers between devices with their start and end apart: 8, of which 4 were waited for; matrix products, arithmetic and copies ran while one was open for 0% of the time, Pallas kernels for 0%

profile of v2, /device:TPU:56, one launch (start us, length us, event | category | flops | bytes accessed | tf_op | source)
XLA Modules:
  0.0 85.8 jit_solution(15985607501240479867)
XLA Ops:
  0.0 0.7 fusion.3
  0.7 0.6 fusion.2
  3.2 1.2 %multiply_bitcast_fusion = (bf16[8,128,128]{2,1,0:T(8,128)(2,1)S(1)}, bf16[8,128,128]{2,1,0:T(8,128)(2,1)S(1)}, bf16[8,128,128]{2,1,0:T(8,128)(2,1)S(1)}, bf16[5,8,128,128]{3,2,1,0:T(8,128)(2,1)S(1)}) fusion(bf16[1,8,128,128]{3,2,1,0:T(8,128)(2,1)} %param.4, bf16[]{:T(256)S(6)} %mul.40, bf16[]{:T(256)S(6)} %mul.36, bf16[]{:T(256)} %bitcast.1), kind=kLoop, calls=%fused_computation.6 | loop fusion | flops 1310719 | bytes 1310726 | tf_op jit(solution)/shard_map/mul | solution.py:143
  4.4 1.9 %collective-permute-start = (bf16[8,128,128]{2,1,0:T(8,128)(2,1)S(1)}, bf16[8,128,128]{2,1,0:T(8,128)(2,1)S(1)}, u32[]{:S(2)}, u32[]{:S(2)}) collective-permute-start(bf16[8,128,128]{2,1,0:T(8,128)(2,1)S(1)} %get-tuple-element.11), channel_id=1, source_target_pairs={{0,4},{4,8},{8,12},{12,16},{16,20},{20,24},{24,28},{28,32},{32,36}... | collective-permute-start | bytes 786440 | tf_op jit(solution)/shard_map/ppermute | solution.py:22
  6.4 10.1 %collective-permute-start.1 = (bf16[8,128,128]{2,1,0:T(8,128)(2,1)S(1)}, bf16[8,128,128]{2,1,0:T(8,128)(2,1)S(1)}, u32[]{:S(2)}, u32[]{:S(2)}) collective-permute-start(bf16[8,128,128]{2,1,0:T(8,128)(2,1)S(1)} %get-tuple-element.11), channel_id=1, source_target_pairs={{0,8},{4,12},{8,16},{12,20},{16,24},{20,28},{24,32},{28,36},{32,40... | collective-permute-start | bytes 786440 | tf_op jit(solution)/shard_map/ppermute | solution.py:22
  16.5 3.4 %collective-permute-start.2 = (bf16[8,128,128]{2,1,0:T(8,128)(2,1)S(1)}, bf16[8,128,128]{2,1,0:T(8,128)(2,1)S(1)}, u32[]{:S(2)}, u32[]{:S(2)}) collective-permute-start(bf16[8,128,128]{2,1,0:T(8,128)(2,1)S(1)} %get-tuple-element.10), channel_id=1, source_target_pairs={{0,508},{4,0},{8,4},{12,8},{16,12},{20,16},{24,20},{28,24},{32,28}... | collective-permute-start | bytes 786440 | tf_op jit(solution)/shard_map/ppermute | solution.py:22
  19.9 1.9 %collective-permute-start.3 = (bf16[8,128,128]{2,1,0:T(8,128)(2,1)S(1)}, bf16[8,128,128]{2,1,0:T(8,128)(2,1)S(1)}, u32[]{:S(2)}, u32[]{:S(2)}) collective-permute-start(bf16[8,128,128]{2,1,0:T(8,128)(2,1)S(1)} %get-tuple-element.9), channel_id=1, source_target_pairs={{0,504},{4,508},{8,0},{12,4},{16,8},{20,12},{24,16},{28,20},{32,24... | collective-permute-start | bytes 786440 | tf_op jit(solution)/shard_map/ppermute | solution.py:22
  21.8 0.0 collective-permute-done
  21.9 6.5 %collective-permute-done.1 = bf16[8,128,128]{2,1,0:T(8,128)(2,1)S(1)} collective-permute-done((bf16[8,128,128]{2,1,0:T(8,128)(2,1)S(1)}, bf16[8,128,128]{2,1,0:T(8,128)(2,1)S(1)}, u32[]{:S(2)}, u32[]{:S(2)}) %collective-permute-start.1) | collective-permute-done | bytes 262176 | tf_op jit(solution)/shard_map/ppermute | solution.py:22
  28.4 0.0 copy-start
  28.4 0.0 collective-permute-done.2
  28.5 18.0 %collective-permute-done.3 = bf16[8,128,128]{2,1,0:T(8,128)(2,1)S(1)} collective-permute-done((bf16[8,128,128]{2,1,0:T(8,128)(2,1)S(1)}, bf16[8,128,128]{2,1,0:T(8,128)(2,1)S(1)}, u32[]{:S(2)}, u32[]{:S(2)}) %collective-permute-start.3) | collective-permute-done | bytes 262176 | tf_op jit(solution)/shard_map/ppermute | solution.py:22
  46.5 0.1 fusion
  46.5 3.8 %collective-permute-start.5 = (bf16[5,2,128,128]{3,2,1,0:T(8,128)(2,1)S(1)}, bf16[5,2,128,128]{3,2,1,0:T(8,128)(2,1)S(1)}, u32[]{:S(2)}, u32[]{:S(2)}) collective-permute-start(bf16[5,2,128,128]{3,2,1,0:T(8,128)(2,1)S(1)} %get-tuple-element.6), channel_id=1, source_target_pairs={{0,3},{1,0},{2,1},{3,2},{4,7},{5,4},{6,5},{7,6},{8,11},{9,8},{10,9... | collective-permute-start | bytes 983048 | tf_op jit(solution)/shard_map/ppermute | solution.py:22
  50.3 2.1 %collective-permute-start.4 = (bf16[5,2,128,128]{3,2,1,0:T(8,128)(2,1)S(1)}, bf16[5,2,128,128]{3,2,1,0:T(8,128)(2,1)S(1)}, u32[]{:S(2)}, u32[]{:S(2)}) collective-permute-start(bf16[5,2,128,128]{3,2,1,0:T(8,128)(2,1)S(1)} %get-tuple-element.5), channel_id=1, source_target_pairs={{0,1},{1,2},{2,3},{3,0},{4,5},{5,6},{6,7},{7,4},{8,9},{9,10},{10,1... | collective-permute-start | bytes 983048 | tf_op jit(solution)/shard_map/ppermute | solution.py:22
  52.4 0.0 copy-done
  52.4 5.6 %collective-permute-start.7 = (f32[2,128,128]{2,1,0:T(8,128)S(1)}, f32[2,128,128]{2,1,0:T(8,128)S(1)}, u32[]{:S(2)}, u32[]{:S(2)}) collective-permute-start(f32[2,128,128]{2,1,0:T(8,128)S(1)} %get-tuple-element.8), channel_id=1, source_target_pairs={{0,3},{1,0},{2,1},{3,2},{4,7},{5,4},{6,5},{7,6},{8,11},{9,8},{10,9... | collective-permute-start | bytes 393224 | tf_op jit(solution)/shard_map/ppermute | solution.py:22
  58.0 1.9 %collective-permute-start.6 = (f32[2,128,128]{2,1,0:T(8,128)S(1)}, f32[2,128,128]{2,1,0:T(8,128)S(1)}, u32[]{:S(2)}, u32[]{:S(2)}) collective-permute-start(f32[2,128,128]{2,1,0:T(8,128)S(1)} %get-tuple-element.7), channel_id=1, source_target_pairs={{0,1},{1,2},{2,3},{3,0},{4,5},{5,6},{6,7},{7,4},{8,9},{9,10},{10,1... | collective-permute-start | bytes 393224 | tf_op jit(solution)/shard_map/ppermute | solution.py:22
  60.0 6.6 %collective-permute-done.7 = f32[2,128,128]{2,1,0:T(8,128)S(1)} collective-permute-done((f32[2,128,128]{2,1,0:T(8,128)S(1)}, f32[2,128,128]{2,1,0:T(8,128)S(1)}, u32[]{:S(2)}, u32[]{:S(2)}) %collective-permute-start.7) | collective-permute-done | bytes 131104 | tf_op jit(solution)/shard_map/ppermute | solution.py:22
  66.6 3.4 %collective-permute-done.6 = f32[2,128,128]{2,1,0:T(8,128)S(1)} collective-permute-done((f32[2,128,128]{2,1,0:T(8,128)S(1)}, f32[2,128,128]{2,1,0:T(8,128)S(1)}, u32[]{:S(2)}, u32[]{:S(2)}) %collective-permute-start.6) | collective-permute-done | bytes 131104 | tf_op jit(solution)/shard_map/ppermute | solution.py:22
  70.0 0.1 pad_maximum_fusion.1.eps_ref
  70.1 0.0 collective-permute-done.5
  70.1 0.0 collective-permute-done.4
  70.1 0.2 pad_maximum_fusion.psi_ref
  70.3 15.4 %shard_map.46 = f32[8,128,128]{2,1,0:T(8,128)} custom-call(f32[4]{0:T(128)S(1)} %concatenate.9.weight_ref, bf16[5,12,128,128]{3,2,1,0:T(8,128)(2,1)S(1)} %pad_maximum_fusion.psi_ref, f32[12,128,128]{2,1,0:T(8,128)S(1)} %pad_maximum_fusion.1.eps_ref), custom_call_target="tpu_custom_call" | custom-call | flops 70778880 | bytes 3276800 | tf_op jit(solution)/shard_map/pallas_call | solution.py:112
  (6 shorter events, 0.2 us)
Async XLA Ops:
  4.4 17.4 %collective-permute-start = (bf16[8,128,128]{2,1,0:T(8,128)(2,1)S(1)}, bf16[8,128,128]{2,1,0:T(8,128)(2,1)S(1)}, u32[]{:S(2)}, u32[]{:S(2)}) collective-permute-start(bf16[8,128,128]{2,1,0:T(8,128)(2,1)S(1)} %get-tuple-element.11), channel_id=1, source_target_pairs={{0,4},{4,8},{8,12},{12,16},{16,20},{20,24},{24,28},{28,32},{32,36}... | collective-permute-start | bytes 786440 | tf_op jit(solution)/shard_map/ppermute | solution.py:22
  6.4 22.0 %collective-permute-start.1 = (bf16[8,128,128]{2,1,0:T(8,128)(2,1)S(1)}, bf16[8,128,128]{2,1,0:T(8,128)(2,1)S(1)}, u32[]{:S(2)}, u32[]{:S(2)}) collective-permute-start(bf16[8,128,128]{2,1,0:T(8,128)(2,1)S(1)} %get-tuple-element.11), channel_id=1, source_target_pairs={{0,8},{4,12},{8,16},{12,20},{16,24},{20,28},{24,32},{28,36},{32,40... | collective-permute-start | bytes 786440 | tf_op jit(solution)/shard_map/ppermute | solution.py:22
  16.5 11.9 %collective-permute-start.2 = (bf16[8,128,128]{2,1,0:T(8,128)(2,1)S(1)}, bf16[8,128,128]{2,1,0:T(8,128)(2,1)S(1)}, u32[]{:S(2)}, u32[]{:S(2)}) collective-permute-start(bf16[8,128,128]{2,1,0:T(8,128)(2,1)S(1)} %get-tuple-element.10), channel_id=1, source_target_pairs={{0,508},{4,0},{8,4},{12,8},{16,12},{20,16},{24,20},{28,24},{32,28}... | collective-permute-start | bytes 786440 | tf_op jit(solution)/shard_map/ppermute | solution.py:22
  19.9 26.6 %collective-permute-start.3 = (bf16[8,128,128]{2,1,0:T(8,128)(2,1)S(1)}, bf16[8,128,128]{2,1,0:T(8,128)(2,1)S(1)}, u32[]{:S(2)}, u32[]{:S(2)}) collective-permute-start(bf16[8,128,128]{2,1,0:T(8,128)(2,1)S(1)} %get-tuple-element.9), channel_id=1, source_target_pairs={{0,504},{4,508},{8,0},{12,4},{16,8},{20,12},{24,16},{28,20},{32,24... | collective-permute-start | bytes 786440 | tf_op jit(solution)/shard_map/ppermute | solution.py:22
  28.4 24.0 %copy-start = (f32[8,128,128]{2,1,0:T(8,128)S(1)}, f32[8,128,128]{2,1,0:T(8,128)}, u32[]{:S(2)}) copy-start(f32[8,128,128]{2,1,0:T(8,128)} %param.5) | copy-start | bytes 1572868
  46.5 23.5 %collective-permute-start.5 = (bf16[5,2,128,128]{3,2,1,0:T(8,128)(2,1)S(1)}, bf16[5,2,128,128]{3,2,1,0:T(8,128)(2,1)S(1)}, u32[]{:S(2)}, u32[]{:S(2)}) collective-permute-start(bf16[5,2,128,128]{3,2,1,0:T(8,128)(2,1)S(1)} %get-tuple-element.6), channel_id=1, source_target_pairs={{0,3},{1,0},{2,1},{3,2},{4,7},{5,4},{6,5},{7,6},{8,11},{9,8},{10,9... | collective-permute-start | bytes 983048 | tf_op jit(solution)/shard_map/ppermute | solution.py:22
  50.3 19.8 %collective-permute-start.4 = (bf16[5,2,128,128]{3,2,1,0:T(8,128)(2,1)S(1)}, bf16[5,2,128,128]{3,2,1,0:T(8,128)(2,1)S(1)}, u32[]{:S(2)}, u32[]{:S(2)}) collective-permute-start(bf16[5,2,128,128]{3,2,1,0:T(8,128)(2,1)S(1)} %get-tuple-element.5), channel_id=1, source_target_pairs={{0,1},{1,2},{2,3},{3,0},{4,5},{5,6},{6,7},{7,4},{8,9},{9,10},{10,1... | collective-permute-start | bytes 983048 | tf_op jit(solution)/shard_map/ppermute | solution.py:22
  52.4 14.2 %collective-permute-start.7 = (f32[2,128,128]{2,1,0:T(8,128)S(1)}, f32[2,128,128]{2,1,0:T(8,128)S(1)}, u32[]{:S(2)}, u32[]{:S(2)}) collective-permute-start(f32[2,128,128]{2,1,0:T(8,128)S(1)} %get-tuple-element.8), channel_id=1, source_target_pairs={{0,3},{1,0},{2,1},{3,2},{4,7},{5,4},{6,5},{7,6},{8,11},{9,8},{10,9... | collective-permute-start | bytes 393224 | tf_op jit(solution)/shard_map/ppermute | solution.py:22
  58.0 12.0 %collective-permute-start.6 = (f32[2,128,128]{2,1,0:T(8,128)S(1)}, f32[2,128,128]{2,1,0:T(8,128)S(1)}, u32[]{:S(2)}, u32[]{:S(2)}) collective-permute-start(f32[2,128,128]{2,1,0:T(8,128)S(1)} %get-tuple-element.7), channel_id=1, source_target_pairs={{0,1},{1,2},{2,3},{3,0},{4,5},{5,6},{6,7},{7,4},{8,9},{9,10},{10,1... | collective-permute-start | bytes 393224 | tf_op jit(solution)/shard_map/ppermute | solution.py:22

commit v3 on v2

--- a/solution.py
+++ b/solution.py
@@ -128,23 +128,44 @@
     )(weights, wide, padded_diel)
 
 
+def exchanged(x, axis, pairs_of):
+    size = lax.axis_size(axis)
+    return lax.ppermute(x, axis, [(i, pairs_of(i) % size) for i in range(size)])
+
+
 def on_device(orbitals, dielectric, occupied, plan):
     psi = orbitals[0]
-    occ = occupied.astype(jnp.bfloat16)[0]
-    flags = plan.astype(jnp.bfloat16).reshape(plan.shape[0])
+    depth, rows, cols = psi.shape
+    ticks = plan.shape[0]
+    flags = plan.astype(jnp.float32).reshape(ticks)
     padded_diel = z_halo(dielectric, 0, HALO)
 
-    ticks = plan.shape[0]
-    lower = psi * occ
-    slabs = [psi]
-    for tick in range(1, ticks + 1):
-        slabs.append(shifted(lower, "band", tick))
-    for tick in range(1, ticks + 1):
-        slabs.append(shifted(psi * (flags[tick - 1] * occ), "band", -tick))
-    wide = z_halo(jnp.stack(slabs), 1, HALO)
-    weights = jnp.concatenate(
-        [plan.astype(jnp.float32).reshape(ticks), jnp.ones((ticks,), jnp.float32)]
+    info = jnp.zeros((16, cols), jnp.bfloat16).at[0, :ticks].set(plan.astype(jnp.bfloat16).reshape(ticks))
+    message = jnp.concatenate(
+        [(psi * occupied.astype(jnp.bfloat16)[0]).reshape(depth * rows, cols), info], axis=0
     )
+    swap = exchanged(message, "band", lambda b: b ^ 1)
+    outer = exchanged(message, "band", lambda b: b + 1 if b % 2 else b - 1)
+    far = exchanged(message, "band", lambda b: b - 2 if b % 2 else b + 2)
+    relay = exchanged(outer, "band", lambda b: b ^ 1)
+
+    def slab(m):
+        return m[: depth * rows].reshape(depth, rows, cols)
+
+    def sent_flags(m):
+        return m[depth * rows, :ticks].astype(jnp.float32)
+
+    odd = lax.axis_index("band") % 2 == 1
+    weights = jnp.stack(
+        [
+            jnp.where(odd, flags[0], sent_flags(swap)[0]),
+            jnp.where(odd, sent_flags(outer)[0], flags[0]),
+            jnp.where(odd, sent_flags(far)[1], flags[1]),
+            jnp.where(odd, flags[1], sent_flags(relay)[1]),
+        ]
+    )
+    stack = jnp.stack([psi, slab(swap), slab(outer), slab(far), slab(relay)])
+    wide = z_halo(stack, 1, HALO)
     return solve(weights, wide, padded_diel)[None]
 
 

time: 86.1 us -> 74.2 us (0.86)
  the two profiles are of different devices: /device:TPU:56 before, /device:TPU:6 now
where the time goes in v3:
time: 74.2 us; the launch traced here: 73.6 us
  starting transfers between devices  35.6 us (48%)
  Pallas kernels  15.5 us (21%)
  local copies, waits for them, and re-layouts  6.65 us (9%)
  between operations  6.1 us (8%)
  waiting for transfers between devices  5.53 us (7%)
  other arithmetic  4.26 us (6%)
    ppermute x4, starting transfers between devices, exchanged(): return lax.ppermute(x, axis, [(i, pairs_of(i) % size) for i in range(size)])  20.3 us
    pallas_call x1, Pallas kernels, solve(): pl.pallas_call(solve_kernel, out_shape=jax.ShapeDtypeStruct((layers - 2 *...  15.5 us
    ppermute x4, starting transfers between devices, shifted(): return lax.ppermute(x, axis, [(i, (i + by) % size) for i in range(size)])  15.3 us
    ppermute x4, waiting for transfers between devices, exchanged(): return lax.ppermute(x, axis, [(i, pairs_of(i) % size) for i in range(size)])  5.52 us
    concatenate x2, other arithmetic, z_halo(): return jnp.concatenate([before, x, after], axis=dim)  2.34 us
  transfers between devices with their start and end apart: 8, of which 1 were waited for; matrix products, arithmetic and copies ran while one was open for 9% of the time, Pallas kernels for 0%

profile of v3, /device:TPU:6, one launch (start us, length us, event | category | flops | bytes accessed | tf_op | source)
XLA Modules:
  0.0 73.6 jit_solution(2802468914664765874)
XLA Ops:
  0.7 0.7 convert_bitcast_fusion
  1.5 1.1 %constant_dynamic-update-slice_fusion.4 = (bf16[5,8,128,128]{3,2,1,0:T(8,128)(2,1)S(1)}, bf16[1,8,128,128]{3,2,1,0:T(8,128)(2,1)S(1)}) fusion(bf16[1,8,128,128]{3,2,1,0:T(8,128)(2,1)} %param.6, bf16[]{:T(256)} %bitcast.1), kind=kLoop, calls=%fused_computation.10 | loop fusion | flops 524287 | bytes 786434
  2.6 13.5 %collective-permute-start.1 = (bf16[1040,128]{1,0:T(8,128)(2,1)S(1)}, bf16[1040,128]{1,0:T(8,128)(2,1)S(1)}, u32[]{:S(2)}, u32[]{:S(2)}) collective-permute-start(bf16[1040,128]{1,0:T(8,128)(2,1)S(1)} %fusion.1), channel_id=1, source_target_pairs={{0,508},{4,8},{8,4},{12,16},{16,12},{20,24},{24,20},{28,32},{32,28... | collective-permute-start | bytes 798728 | tf_op jit(solution)/shard_map/ppermute | solution.py:133
  16.1 1.9 %collective-permute-start = (bf16[1040,128]{1,0:T(8,128)(2,1)S(1)}, bf16[1040,128]{1,0:T(8,128)(2,1)S(1)}, u32[]{:S(2)}, u32[]{:S(2)}) collective-permute-start(bf16[1040,128]{1,0:T(8,128)(2,1)S(1)} %fusion.1), channel_id=1, source_target_pairs={{0,4},{4,0},{8,12},{12,8},{16,20},{20,16},{24,28},{28,24},{32,36},... | collective-permute-start | bytes 798728 | tf_op jit(solution)/shard_map/ppermute | solution.py:133
  18.0 1.9 %collective-permute-start.2 = (bf16[1040,128]{1,0:T(8,128)(2,1)S(1)}, bf16[1040,128]{1,0:T(8,128)(2,1)S(1)}, u32[]{:S(2)}, u32[]{:S(2)}) collective-permute-start(bf16[1040,128]{1,0:T(8,128)(2,1)S(1)} %fusion.1), channel_id=1, source_target_pairs={{0,8},{4,508},{8,16},{12,4},{16,24},{20,12},{24,32},{28,20},{32,40... | collective-permute-start | bytes 798728 | tf_op jit(solution)/shard_map/ppermute | solution.py:133
  20.0 3.4 %collective-permute-start.6 = (f32[2,128,128]{2,1,0:T(8,128)S(1)}, f32[2,128,128]{2,1,0:T(8,128)S(1)}, u32[]{:S(2)}, u32[]{:S(2)}) collective-permute-start(f32[2,128,128]{2,1,0:T(8,128)S(1)} %get-tuple-element.19), channel_id=1, source_target_pairs={{0,1},{1,2},{2,3},{3,0},{4,5},{5,6},{6,7},{7,4},{8,9},{9,10},{10,1... | collective-permute-start | bytes 393224 | tf_op jit(solution)/shard_map/ppermute | solution.py:22
  23.4 4.3 %collective-permute-start.7 = (f32[2,128,128]{2,1,0:T(8,128)S(1)}, f32[2,128,128]{2,1,0:T(8,128)}, u32[]{:S(2)}, u32[]{:S(2)}) collective-permute-start(f32[2,128,128]{2,1,0:T(8,128)S(1)} %get-tuple-element.20), channel_id=1, source_target_pairs={{0,3},{1,0},{2,1},{3,2},{4,7},{5,4},{6,5},{7,6},{8,11},{9,8},{10,9... | collective-permute-start | bytes 393224 | tf_op jit(solution)/shard_map/ppermute | solution.py:22
  27.7 0.0 collective-permute-done.1
  27.7 2.9 %collective-permute-start.3 = (bf16[1040,128]{1,0:T(8,128)(2,1)S(1)}, bf16[1040,128]{1,0:T(8,128)(2,1)S(1)}, u32[]{:S(2)}, u32[]{:S(2)}) collective-permute-start(bf16[1040,128]{1,0:T(8,128)(2,1)S(1)} %collective-permute-done.1), channel_id=1, source_target_pairs={{0,4},{4,0},{8,12},{12,8},{16,20},{20,16},{24,28},{28,24},{32,36},... | collective-permute-start | bytes 798728 | tf_op jit(solution)/shard_map/ppermute | solution.py:133
  30.6 0.0 collective-permute-done
  30.6 0.0 copy-start.2
  30.7 5.5 %collective-permute-done.2 = bf16[1040,128]{1,0:T(8,128)(2,1)S(1)} collective-permute-done((bf16[1040,128]{1,0:T(8,128)(2,1)S(1)}, bf16[1040,128]{1,0:T(8,128)(2,1)S(1)}, u32[]{:S(2)}, u32[]{:S(2)}) %collective-permute-start.2) | collective-permute-done | bytes 266272 | tf_op jit(solution)/shard_map/ppermute | solution.py:133
  36.4 0.0 collective-permute-done.3
  36.4 0.0 copy-start.3
  36.4 0.5 copy-done.1
  36.9 0.1 copy-done.3
  37.2 2.0 %collective-permute-start.4 = (bf16[5,2,128,128]{3,2,1,0:T(8,128)(2,1)S(1)}, bf16[5,2,128,128]{3,2,1,0:T(8,128)(2,1)}, u32[]{:S(2)}, u32[]{:S(2)}) collective-permute-start(bf16[5,2,128,128]{3,2,1,0:T(8,128)(2,1)S(1)} %get-tuple-element.17), channel_id=1, source_target_pairs={{0,1},{1,2},{2,3},{3,0},{4,5},{5,6},{6,7},{7,4},{8,9},{9,10},{10,1... | collective-permute-start | bytes 983048 | tf_op jit(solution)/shard_map/ppermute | solution.py:22
  39.1 5.7 %collective-permute-start.5 = (bf16[5,2,128,128]{3,2,1,0:T(8,128)(2,1)S(1)}, bf16[5,2,128,128]{3,2,1,0:T(8,128)(2,1)}, u32[]{:S(2)}, u32[]{:S(2)}) collective-permute-start(bf16[5,2,128,128]{3,2,1,0:T(8,128)(2,1)S(1)} %get-tuple-element.18), channel_id=1, source_target_pairs={{0,3},{1,0},{2,1},{3,2},{4,7},{5,4},{6,5},{7,6},{8,11},{9,8},{10,9... | collective-permute-start | bytes 983048 | tf_op jit(solution)/shard_map/ppermute | solution.py:22
  44.8 0.6 fusion.4
  45.4 0.0 collective-permute-done.6
  45.4 0.6 copy-done.4
  46.1 0.0 collective-permute-done.7
  46.1 1.0 %pad_maximum_fusion.1.eps_ref = f32[12,128,128]{2,1,0:T(8,128)S(1)} fusion(f32[2,128,128]{2,1,0:T(8,128)} %collective-permute-done.7, f32[8,128,128]{2,1,0:T(8,128)S(1)} %copy-done, f32[2,128,128]{2,1,0:T(8,128)} %copy-done.4), kind=kLoop, calls=%fused_computation.1 | loop fusion | flops 393216 | bytes 1572864 | tf_op jit(solution)/shard_map/concatenate | solution.py:31
  47.1 1.2 %slice.92 = bf16[1,1]{1,0:T(2,128)(2,1)} slice(bf16[1040,128]{1,0:T(8,128)(2,1)} %copy-done.2), slice={[1024:1025], [0:1]} | slice | bytes 4 | tf_op jit(solution)/shard_map/slice | solution.py:161
  49.6 0.6 slice.93
  51.5 1.3 %slice.94 = bf16[1,1]{1,0:T(2,128)(2,1)} slice(bf16[1040,128]{1,0:T(8,128)(2,1)} %copy-done.1), slice={[1024:1025], [1:2]} | slice | bytes 4 | tf_op jit(solution)/shard_map/slice | solution.py:163
  54.1 1.3 %slice.95 = bf16[1,1]{1,0:T(2,128)(2,1)} slice(bf16[1040,128]{1,0:T(8,128)(2,1)} %copy-done.3), slice={[1024:1025], [1:2]} | slice | bytes 4 | tf_op jit(solution)/shard_map/slice | solution.py:164
  56.7 0.1 pad_maximum_fusion.2.weight_ref
  56.8 0.0 collective-permute-done.4
  56.8 0.0 collective-permute-done.5
  56.8 1.3 %pad_maximum_fusion.psi_ref = bf16[5,12,128,128]{3,2,1,0:T(8,128)(2,1)S(1)} fusion(bf16[5,2,128,128]{3,2,1,0:T(8,128)(2,1)} %collective-permute-done.5, bf16[5,8,128,128]{3,2,1,0:T(8,128)(2,1)S(1)} %constant_dynamic-update-slice_fusion, bf16[5,2,128,128]{3,2,1,0:T(8,128)(2,1)} %collective-permute-done.4), kind=kLoop, calls=%fused_computation | loop fusion | flops 1966080 | bytes 3932160 | tf_op jit(solution)/shard_map/concatenate | solution.py:31
  58.1 15.5 %shard_map.46 = f32[8,128,128]{2,1,0:T(8,128)} custom-call(f32[4]{0:T(128)S(1)} %pad_maximum_fusion.2.weight_ref, bf16[5,12,128,128]{3,2,1,0:T(8,128)(2,1)S(1)} %pad_maximum_fusion.psi_ref, f32[12,128,128]{2,1,0:T(8,128)S(1)} %pad_maximum_fusion.1.eps_ref), custom_call_target="tpu_custom_call" | custom-call | flops 70778880 | bytes 3276800 | tf_op jit(solution)/shard_map/pallas_call | solution.py:112
  (16 shorter events, 0.3 us)
Async XLA Ops:
  0.0 20.0 %copy-start = (f32[8,128,128]{2,1,0:T(8,128)S(1)}, f32[8,128,128]{2,1,0:T(8,128)}, u32[]{:S(2)}) copy-start(f32[8,128,128]{2,1,0:T(8,128)} %param.7) | copy-start | bytes 1572868
  2.6 25.1 %collective-permute-start.1 = (bf16[1040,128]{1,0:T(8,128)(2,1)S(1)}, bf16[1040,128]{1,0:T(8,128)(2,1)S(1)}, u32[]{:S(2)}, u32[]{:S(2)}) collective-permute-start(bf16[1040,128]{1,0:T(8,128)(2,1)S(1)} %fusion.1), channel_id=1, source_target_pairs={{0,508},{4,8},{8,4},{12,16},{16,12},{20,24},{24,20},{28,32},{32,28... | collective-permute-start | bytes 798728 | tf_op jit(solution)/shard_map/ppermute | solution.py:133
  16.1 14.5 %collective-permute-start = (bf16[1040,128]{1,0:T(8,128)(2,1)S(1)}, bf16[1040,128]{1,0:T(8,128)(2,1)S(1)}, u32[]{:S(2)}, u32[]{:S(2)}) collective-permute-start(bf16[1040,128]{1,0:T(8,128)(2,1)S(1)} %fusion.1), channel_id=1, source_target_pairs={{0,4},{4,0},{8,12},{12,8},{16,20},{20,16},{24,28},{28,24},{32,36},... | collective-permute-start | bytes 798728 | tf_op jit(solution)/shard_map/ppermute | solution.py:133
  18.0 18.2 %collective-permute-start.2 = (bf16[1040,128]{1,0:T(8,128)(2,1)S(1)}, bf16[1040,128]{1,0:T(8,128)(2,1)S(1)}, u32[]{:S(2)}, u32[]{:S(2)}) collective-permute-start(bf16[1040,128]{1,0:T(8,128)(2,1)S(1)} %fusion.1), channel_id=1, source_target_pairs={{0,8},{4,508},{8,16},{12,4},{16,24},{20,12},{24,32},{28,20},{32,40... | collective-permute-start | bytes 798728 | tf_op jit(solution)/shard_map/ppermute | solution.py:133
  20.0 25.4 %collective-permute-start.6 = (f32[2,128,128]{2,1,0:T(8,128)S(1)}, f32[2,128,128]{2,1,0:T(8,128)S(1)}, u32[]{:S(2)}, u32[]{:S(2)}) collective-permute-start(f32[2,128,128]{2,1,0:T(8,128)S(1)} %get-tuple-element.19), channel_id=1, source_target_pairs={{0,1},{1,2},{2,3},{3,0},{4,5},{5,6},{6,7},{7,4},{8,9},{9,10},{10,1... | collective-permute-start | bytes 393224 | tf_op jit(solution)/shard_map/ppermute | solution.py:22
  23.4 22.7 %collective-permute-start.7 = (f32[2,128,128]{2,1,0:T(8,128)S(1)}, f32[2,128,128]{2,1,0:T(8,128)}, u32[]{:S(2)}, u32[]{:S(2)}) collective-permute-start(f32[2,128,128]{2,1,0:T(8,128)S(1)} %get-tuple-element.20), channel_id=1, source_target_pairs={{0,3},{1,0},{2,1},{3,2},{4,7},{5,4},{6,5},{7,6},{8,11},{9,8},{10,9... | collective-permute-start | bytes 393224 | tf_op jit(solution)/shard_map/ppermute | solution.py:22
  27.7 8.7 %collective-permute-start.3 = (bf16[1040,128]{1,0:T(8,128)(2,1)S(1)}, bf16[1040,128]{1,0:T(8,128)(2,1)S(1)}, u32[]{:S(2)}, u32[]{:S(2)}) collective-permute-start(bf16[1040,128]{1,0:T(8,128)(2,1)S(1)} %collective-permute-done.1), channel_id=1, source_target_pairs={{0,4},{4,0},{8,12},{12,8},{16,20},{20,16},{24,28},{28,24},{32,36},... | collective-permute-start | bytes 798728 | tf_op jit(solution)/shard_map/ppermute | solution.py:133
  30.6 5.7 %copy-start.2 = (bf16[1040,128]{1,0:T(8,128)(2,1)}, bf16[1040,128]{1,0:T(8,128)(2,1)S(1)}, u32[]{:S(2)}) copy-start(bf16[1040,128]{1,0:T(8,128)(2,1)S(1)} %collective-permute-done) | copy-start | bytes 798724
  36.2 0.7 copy-start.1
  36.4 0.7 copy-start.3
  37.2 19.6 %collective-permute-start.4 = (bf16[5,2,128,128]{3,2,1,0:T(8,128)(2,1)S(1)}, bf16[5,2,128,128]{3,2,1,0:T(8,128)(2,1)}, u32[]{:S(2)}, u32[]{:S(2)}) collective-permute-start(bf16[5,2,128,128]{3,2,1,0:T(8,128)(2,1)S(1)} %get-tuple-element.17), channel_id=1, source_target_pairs={{0,1},{1,2},{2,3},{3,0},{4,5},{5,6},{6,7},{7,4},{8,9},{9,10},{10,1... | collective-permute-start | bytes 983048 | tf_op jit(solution)/shard_map/ppermute | solution.py:22
  39.1 17.7 %collective-permute-start.5 = (bf16[5,2,128,128]{3,2,1,0:T(8,128)(2,1)S(1)}, bf16[5,2,128,128]{3,2,1,0:T(8,128)(2,1)}, u32[]{:S(2)}, u32[]{:S(2)}) collective-permute-start(bf16[5,2,128,128]{3,2,1,0:T(8,128)(2,1)S(1)} %get-tuple-element.18), channel_id=1, source_target_pairs={{0,3},{1,0},{2,1},{3,2},{4,7},{5,4},{6,5},{7,6},{8,11},{9,8},{10,9... | collective-permute-start | bytes 983048 | tf_op jit(solution)/shard_map/ppermute | solution.py:22
  45.4 0.6 copy-start.4

commit v4 on v3

--- a/solution.py
+++ b/solution.py
@@ -113,7 +113,7 @@
         solve_kernel,
         out_shape=jax.ShapeDtypeStruct((layers - 2 * HALO, rows, cols), jnp.float32),
         in_specs=[
-            pl.BlockSpec(memory_space=pltpu.SMEM),
+            pl.BlockSpec(memory_space=vmem),
             pl.BlockSpec(memory_space=vmem),
             pl.BlockSpec(memory_space=vmem),
         ],
@@ -140,7 +140,9 @@
     flags = plan.astype(jnp.float32).reshape(ticks)
     padded_diel = z_halo(dielectric, 0, HALO)
 
-    info = jnp.zeros((16, cols), jnp.bfloat16).at[0, :ticks].set(plan.astype(jnp.bfloat16).reshape(ticks))
+    info = jnp.zeros((16, cols), jnp.bfloat16).at[:ticks, :].set(
+        jnp.broadcast_to(plan.astype(jnp.bfloat16).reshape(ticks, 1), (ticks, cols))
+    )
     message = jnp.concatenate(
         [(psi * occupied.astype(jnp.bfloat16)[0]).reshape(depth * rows, cols), info], axis=0
     )
@@ -152,16 +154,19 @@
     def slab(m):
         return m[: depth * rows].reshape(depth, rows, cols)
 
-    def sent_flags(m):
-        return m[depth * rows, :ticks].astype(jnp.float32)
+    def sent_flags(m, tick):
+        return m[depth * rows + tick : depth * rows + tick + 1].astype(jnp.float32)
+
+    def own_flags(tick):
+        return jnp.broadcast_to(flags[tick], (1, cols))
 
     odd = lax.axis_index("band") % 2 == 1
     weights = jnp.stack(
         [
-            jnp.where(odd, flags[0], sent_flags(swap)[0]),
-            jnp.where(odd, sent_flags(outer)[0], flags[0]),
-            jnp.where(odd, sent_flags(far)[1], flags[1]),
-            jnp.where(odd, flags[1], sent_flags(relay)[1]),
+            jnp.where(odd, own_flags(0), sent_flags(swap, 0)),
+            jnp.where(odd, sent_flags(outer, 0), own_flags(0)),
+            jnp.where(odd, sent_flags(far, 1), own_flags(1)),
+            jnp.where(odd, own_flags(1), sent_flags(relay, 1)),
         ]
     )
     stack = jnp.stack([psi, slab(swap), slab(outer), slab(far), slab(relay)])

time: 74.2 us -> 74.2 us (level)
  the two profiles are of different devices: /device:TPU:6 before, /device:TPU:64 now
where the time goes in v4:
time: 74.2 us; the launch traced here: 73.8 us
  starting transfers between devices  32.6 us (44%)
  waiting for transfers between devices  19.8 us (27%)
  Pallas kernels  14.9 us (20%)
  other arithmetic  4.75 us (6%)
  between operations  0.94 us (1%)
  local copies, waits for them, and re-layouts  0.88 us (1%)
    ppermute x4, starting transfers between devices, exchanged(): return lax.ppermute(x, axis, [(i, pairs_of(i) % size) for i in range(size)])  17.4 us
    ppermute x4, starting transfers between devices, shifted(): return lax.ppermute(x, axis, [(i, (i + by) % size) for i in range(size)])  15.1 us
    pallas_call x1, Pallas kernels, solve(): pl.pallas_call(solve_kernel, out_shape=jax.ShapeDtypeStruct((layers - 2 *...  14.9 us
    ppermute x4, waiting for transfers between devices, exchanged(): return lax.ppermute(x, axis, [(i, pairs_of(i) % size) for i in range(size)])  11.4 us
    ppermute x4, waiting for transfers between devices, shifted(): return lax.ppermute(x, axis, [(i, (i + by) % size) for i in range(size)])  8.39 us
    another operation x5, other arithmetic, on_device(): jnp.stack([jnp.where(odd, own_flags(0), sent_flags(swap, 0)), jnp.where(o...  2.44 us
  transfers between devices with their start and end apart: 8, of which 4 were waited for; matrix products, arithmetic and copies ran while one was open for 4% of the time, Pallas kernels for 0%

profile of v4, /device:TPU:64, one launch (start us, length us, event | category | flops | bytes accessed | tf_op | source)
XLA Modules:
  0.0 73.8 jit_solution(12539813013599564025)
XLA Ops:
  0.0 0.0 copy-start
  0.7 0.7 fusion.8
  1.5 1.1 %constant_dynamic-update-slice_fusion.4 = (bf16[5,8,128,128]{3,2,1,0:T(8,128)(2,1)S(1)}, bf16[1,8,128,128]{3,2,1,0:T(8,128)(2,1)S(1)}) fusion(bf16[1,8,128,128]{3,2,1,0:T(8,128)(2,1)} %param.6, bf16[]{:T(256)} %bitcast.1), kind=kLoop, calls=%fused_computation.8 | loop fusion | flops 524287 | bytes 786434
  2.6 0.2 pad_maximum_fusion.2
  2.8 1.9 %collective-permute-start = (bf16[1040,128]{1,0:T(8,128)(2,1)S(1)}, bf16[1040,128]{1,0:T(8,128)(2,1)S(1)}, u32[]{:S(2)}, u32[]{:S(2)}) collective-permute-start(bf16[1040,128]{1,0:T(8,128)(2,1)S(1)} %pad_maximum_fusion.2), channel_id=1, source_target_pairs={{0,4},{4,0},{8,12},{12,8},{16,20},{20,16},{24,28},{28,24},{32,36},... | collective-permute-start | bytes 798728 | tf_op jit(solution)/shard_map/ppermute | solution.py:133
  4.7 0.0 copy-done
  4.7 4.3 %collective-permute-start.6 = (f32[2,128,128]{2,1,0:T(8,128)S(1)}, f32[2,128,128]{2,1,0:T(8,128)S(1)}, u32[]{:S(2)}, u32[]{:S(2)}) collective-permute-start(f32[2,128,128]{2,1,0:T(8,128)S(1)} %get-tuple-element.19), channel_id=1, source_target_pairs={{0,1},{1,2},{2,3},{3,0},{4,5},{5,6},{6,7},{7,4},{8,9},{9,10},{10,1... | collective-permute-start | bytes 393224 | tf_op jit(solution)/shard_map/ppermute | solution.py:22
  9.0 4.5 %collective-permute-start.7 = (f32[2,128,128]{2,1,0:T(8,128)S(1)}, f32[2,128,128]{2,1,0:T(8,128)S(1)}, u32[]{:S(2)}, u32[]{:S(2)}) collective-permute-start(f32[2,128,128]{2,1,0:T(8,128)S(1)} %get-tuple-element.20), channel_id=1, source_target_pairs={{0,3},{1,0},{2,1},{3,2},{4,7},{5,4},{6,5},{7,6},{8,11},{9,8},{10,9... | collective-permute-start | bytes 393224 | tf_op jit(solution)/shard_map/ppermute | solution.py:22
  13.6 11.7 %collective-permute-start.1 = (bf16[1040,128]{1,0:T(8,128)(2,1)S(1)}, bf16[1040,128]{1,0:T(8,128)(2,1)S(1)}, u32[]{:S(2)}, u32[]{:S(2)}) collective-permute-start(bf16[1040,128]{1,0:T(8,128)(2,1)S(1)} %pad_maximum_fusion.2), channel_id=1, source_target_pairs={{0,508},{4,8},{8,4},{12,16},{16,12},{20,24},{24,20},{28,32},{32,28... | collective-permute-start | bytes 798728 | tf_op jit(solution)/shard_map/ppermute | solution.py:133
  25.3 1.9 %collective-permute-start.2 = (bf16[1040,128]{1,0:T(8,128)(2,1)S(1)}, bf16[1040,128]{1,0:T(8,128)(2,1)S(1)}, u32[]{:S(2)}, u32[]{:S(2)}) collective-permute-start(bf16[1040,128]{1,0:T(8,128)(2,1)S(1)} %pad_maximum_fusion.2), channel_id=1, source_target_pairs={{0,8},{4,508},{8,16},{12,4},{16,24},{20,12},{24,32},{28,20},{32,40... | collective-permute-start | bytes 798728 | tf_op jit(solution)/shard_map/ppermute | solution.py:133
  27.2 0.6 fusion.7
  27.8 0.0 collective-permute-done.6
  27.8 0.0 collective-permute-done.7
  27.8 0.1 pad_maximum_fusion.1.eps_ref
  27.8 0.0 collective-permute-done
  27.9 3.2 %collective-permute-done.1 = bf16[1040,128]{1,0:T(8,128)(2,1)S(1)} collective-permute-done((bf16[1040,128]{1,0:T(8,128)(2,1)S(1)}, bf16[1040,128]{1,0:T(8,128)(2,1)S(1)}, u32[]{:S(2)}, u32[]{:S(2)}) %collective-permute-start.1) | collective-permute-done | bytes 266272 | tf_op jit(solution)/shard_map/ppermute | solution.py:133
  31.1 1.9 %collective-permute-start.3 = (bf16[1040,128]{1,0:T(8,128)(2,1)S(1)}, bf16[1040,128]{1,0:T(8,128)(2,1)S(1)}, u32[]{:S(2)}, u32[]{:S(2)}) collective-permute-start(bf16[1040,128]{1,0:T(8,128)(2,1)S(1)} %collective-permute-done.1), channel_id=1, source_target_pairs={{0,4},{4,0},{8,12},{12,8},{16,20},{20,16},{24,28},{28,24},{32,36},... | collective-permute-start | bytes 798728 | tf_op jit(solution)/shard_map/ppermute | solution.py:133
  33.1 0.7 fusion.1
  33.8 0.7 fusion.2
  34.4 8.2 %collective-permute-done.2 = bf16[1040,128]{1,0:T(8,128)(2,1)S(1)} collective-permute-done((bf16[1040,128]{1,0:T(8,128)(2,1)S(1)}, bf16[1040,128]{1,0:T(8,128)(2,1)S(1)}, u32[]{:S(2)}, u32[]{:S(2)}) %collective-permute-start.2) | collective-permute-done | bytes 266272 | tf_op jit(solution)/shard_map/ppermute | solution.py:133
  42.7 0.6 fusion.3
  43.3 0.0 collective-permute-done.3
  43.4 3.4 %collective-permute-start.4 = (bf16[5,2,128,128]{3,2,1,0:T(8,128)(2,1)S(1)}, bf16[5,2,128,128]{3,2,1,0:T(8,128)(2,1)S(1)}, u32[]{:S(2)}, u32[]{:S(2)}) collective-permute-start(bf16[5,2,128,128]{3,2,1,0:T(8,128)(2,1)S(1)} %get-tuple-element.17), channel_id=1, source_target_pairs={{0,1},{1,2},{2,3},{3,0},{4,5},{5,6},{6,7},{7,4},{8,9},{9,10},{10,1... | collective-permute-start | bytes 983048 | tf_op jit(solution)/shard_map/ppermute | solution.py:22
  46.8 2.9 %collective-permute-start.5 = (bf16[5,2,128,128]{3,2,1,0:T(8,128)(2,1)S(1)}, bf16[5,2,128,128]{3,2,1,0:T(8,128)(2,1)S(1)}, u32[]{:S(2)}, u32[]{:S(2)}) collective-permute-start(bf16[5,2,128,128]{3,2,1,0:T(8,128)(2,1)S(1)} %get-tuple-element.18), channel_id=1, source_target_pairs={{0,3},{1,0},{2,1},{3,2},{4,7},{5,4},{6,5},{7,6},{8,11},{9,8},{10,9... | collective-permute-start | bytes 983048 | tf_op jit(solution)/shard_map/ppermute | solution.py:22
  49.7 0.6 fusion.4
  50.3 3.9 %collective-permute-done.4 = bf16[5,2,128,128]{3,2,1,0:T(8,128)(2,1)S(1)} collective-permute-done((bf16[5,2,128,128]{3,2,1,0:T(8,128)(2,1)S(1)}, bf16[5,2,128,128]{3,2,1,0:T(8,128)(2,1)S(1)}, u32[]{:S(2)}, u32[]{:S(2)}) %collective-permute-start.4) | collective-permute-done | bytes 327712 | tf_op jit(solution)/shard_map/ppermute | solution.py:22
  54.2 4.5 %collective-permute-done.5 = bf16[5,2,128,128]{3,2,1,0:T(8,128)(2,1)S(1)} collective-permute-done((bf16[5,2,128,128]{3,2,1,0:T(8,128)(2,1)S(1)}, bf16[5,2,128,128]{3,2,1,0:T(8,128)(2,1)S(1)}, u32[]{:S(2)}, u32[]{:S(2)}) %collective-permute-start.5) | collective-permute-done | bytes 327712 | tf_op jit(solution)/shard_map/ppermute | solution.py:22
  58.7 0.2 pad_maximum_fusion.psi_ref
  58.9 14.9 %shard_map.46 = f32[8,128,128]{2,1,0:T(8,128)} custom-call(f32[4,1,128]{2,1,0:T(1,128)S(1)} %pad_maximum_fusion.3.weight_ref, bf16[5,12,128,128]{3,2,1,0:T(8,128)(2,1)S(1)} %pad_maximum_fusion.psi_ref, f32[12,128,128]{2,1,0:T(8,128)S(1)} %pad_maximum_fusion.1.eps_ref), custom_call_target="tpu_custom_call" | custom-call | flops 70778880 | bytes 3276800 | tf_op jit(solution)/shard_map/pallas_call | solution.py:112
  (12 shorter events, 0.3 us)
Async XLA Ops:
  0.0 4.7 %copy-start = (f32[8,128,128]{2,1,0:T(8,128)S(1)}, f32[8,128,128]{2,1,0:T(8,128)}, u32[]{:S(2)}) copy-start(f32[8,128,128]{2,1,0:T(8,128)} %param.7) | copy-start | bytes 1572868
  2.8 25.1 %collective-permute-start = (bf16[1040,128]{1,0:T(8,128)(2,1)S(1)}, bf16[1040,128]{1,0:T(8,128)(2,1)S(1)}, u32[]{:S(2)}, u32[]{:S(2)}) collective-permute-start(bf16[1040,128]{1,0:T(8,128)(2,1)S(1)} %pad_maximum_fusion.2), channel_id=1, source_target_pairs={{0,4},{4,0},{8,12},{12,8},{16,20},{20,16},{24,28},{28,24},{32,36},... | collective-permute-start | bytes 798728 | tf_op jit(solution)/shard_map/ppermute | solution.py:133
  4.7 23.0 %collective-permute-start.6 = (f32[2,128,128]{2,1,0:T(8,128)S(1)}, f32[2,128,128]{2,1,0:T(8,128)S(1)}, u32[]{:S(2)}, u32[]{:S(2)}) collective-permute-start(f32[2,128,128]{2,1,0:T(8,128)S(1)} %get-tuple-element.19), channel_id=1, source_target_pairs={{0,1},{1,2},{2,3},{3,0},{4,5},{5,6},{6,7},{7,4},{8,9},{9,10},{10,1... | collective-permute-start | bytes 393224 | tf_op jit(solution)/shard_map/ppermute | solution.py:22
  9.0 18.8 %collective-permute-start.7 = (f32[2,128,128]{2,1,0:T(8,128)S(1)}, f32[2,128,128]{2,1,0:T(8,128)S(1)}, u32[]{:S(2)}, u32[]{:S(2)}) collective-permute-start(f32[2,128,128]{2,1,0:T(8,128)S(1)} %get-tuple-element.20), channel_id=1, source_target_pairs={{0,3},{1,0},{2,1},{3,2},{4,7},{5,4},{6,5},{7,6},{8,11},{9,8},{10,9... | collective-permute-start | bytes 393224 | tf_op jit(solution)/shard_map/ppermute | solution.py:22
  13.6 17.6 %collective-permute-start.1 = (bf16[1040,128]{1,0:T(8,128)(2,1)S(1)}, bf16[1040,128]{1,0:T(8,128)(2,1)S(1)}, u32[]{:S(2)}, u32[]{:S(2)}) collective-permute-start(bf16[1040,128]{1,0:T(8,128)(2,1)S(1)} %pad_maximum_fusion.2), channel_id=1, source_target_pairs={{0,508},{4,8},{8,4},{12,16},{16,12},{20,24},{24,20},{28,32},{32,28... | collective-permute-start | bytes 798728 | tf_op jit(solution)/shard_map/ppermute | solution.py:133
  25.3 17.4 %collective-permute-start.2 = (bf16[1040,128]{1,0:T(8,128)(2,1)S(1)}, bf16[1040,128]{1,0:T(8,128)(2,1)S(1)}, u32[]{:S(2)}, u32[]{:S(2)}) collective-permute-start(bf16[1040,128]{1,0:T(8,128)(2,1)S(1)} %pad_maximum_fusion.2), channel_id=1, source_target_pairs={{0,8},{4,508},{8,16},{12,4},{16,24},{20,12},{24,32},{28,20},{32,40... | collective-permute-start | bytes 798728 | tf_op jit(solution)/shard_map/ppermute | solution.py:133
  31.1 12.1 %collective-permute-start.3 = (bf16[1040,128]{1,0:T(8,128)(2,1)S(1)}, bf16[1040,128]{1,0:T(8,128)(2,1)S(1)}, u32[]{:S(2)}, u32[]{:S(2)}) collective-permute-start(bf16[1040,128]{1,0:T(8,128)(2,1)S(1)} %collective-permute-done.1), channel_id=1, source_target_pairs={{0,4},{4,0},{8,12},{12,8},{16,20},{20,16},{24,28},{28,24},{32,36},... | collective-permute-start | bytes 798728 | tf_op jit(solution)/shard_map/ppermute | solution.py:133
  43.4 10.8 %collective-permute-start.4 = (bf16[5,2,128,128]{3,2,1,0:T(8,128)(2,1)S(1)}, bf16[5,2,128,128]{3,2,1,0:T(8,128)(2,1)S(1)}, u32[]{:S(2)}, u32[]{:S(2)}) collective-permute-start(bf16[5,2,128,128]{3,2,1,0:T(8,128)(2,1)S(1)} %get-tuple-element.17), channel_id=1, source_target_pairs={{0,1},{1,2},{2,3},{3,0},{4,5},{5,6},{6,7},{7,4},{8,9},{9,10},{10,1... | collective-permute-start | bytes 983048 | tf_op jit(solution)/shard_map/ppermute | solution.py:22
  46.8 11.9 %collective-permute-start.5 = (bf16[5,2,128,128]{3,2,1,0:T(8,128)(2,1)S(1)}, bf16[5,2,128,128]{3,2,1,0:T(8,128)(2,1)S(1)}, u32[]{:S(2)}, u32[]{:S(2)}) collective-permute-start(bf16[5,2,128,128]{3,2,1,0:T(8,128)(2,1)S(1)} %get-tuple-element.18), channel_id=1, source_target_pairs={{0,3},{1,0},{2,1},{3,2},{4,7},{5,4},{6,5},{7,6},{8,11},{9,8},{10,9... | collective-permute-start | bytes 983048 | tf_op jit(solution)/shard_map/ppermute | solution.py:22

commit v5 on v4

--- a/solution.py
+++ b/solution.py
@@ -1,3 +1,4 @@
+import functools
 import math
 
 import jax
@@ -31,28 +32,15 @@
     return jnp.concatenate([before, x, after], axis=dim)
 
 
-def solve_kernel(weight_ref, psi_ref, eps_ref, out_ref, face_z, face_x, face_y, dens, first, rem, second, partial):
-    layers, rows, cols = eps_ref.shape
+def solve_kernel(windows, weight_ref, psi_ref, eps_ref, out_ref, face_z, face_x, face_y, dens, first, rem, second, partial, flux):
+    _, rows, cols = eps_ref.shape
     pairs = psi_ref.shape[0] - 1
-
-    def faces(e, carry):
-        cur = eps_ref[e]
-        face_x[e] = (cur + pltpu.roll(cur, rows - 1, 0)) * 0.5
-        face_y[e] = (cur + pltpu.roll(cur, cols - 1, 1)) * 0.5
-        return carry
-
-    lax.fori_loop(0, layers, faces, 0)
-
-    def faces_z(e, carry):
-        face_z[e] = (eps_ref[e] + eps_ref[e + 1]) * 0.5
-        return carry
-
-    lax.fori_loop(0, layers - 1, faces_z, 0)
 
     def applied(field, e):
         center = field[e]
         flux_up = face_z[e] * (field[e + 1] - center)
-        flux_down = face_z[e - 1] * (center - field[e - 1])
+        flux_down = flux[...]
+        flux[...] = flux_up
         part_z = flux_up - flux_down
         flux_x = face_x[e] * (pltpu.roll(center, rows - 1, 0) - center)
         part_x = flux_x - pltpu.roll(flux_x, 1, 0)
@@ -68,64 +56,78 @@
     keep_two, mix_two = factor_two * factor_one, 2.0 * factor_two / CHEB_HALF
 
     out_ref[...] = jnp.zeros(out_ref.shape, out_ref.dtype)
-    for k in range(pairs):
-        weight = weight_ref[k]
+    out_at = 0
+    for start, size in windows:
 
-        def density(e, carry):
-            own = psi_ref[0, e].astype(jnp.float32)
-            partner = psi_ref[k + 1, e].astype(jnp.float32)
-            value = (FOUR_PI * own) * partner
-            dens[e] = value
-            first[e] = value / CHEB_CENTER
+        def faces(e, carry):
+            cur = eps_ref[start + e]
+            face_x[e] = (cur + pltpu.roll(cur, rows - 1, 0)) * 0.5
+            face_y[e] = (cur + pltpu.roll(cur, cols - 1, 1)) * 0.5
+            face_z[e] = (cur + eps_ref[start + e + 1]) * 0.5
             return carry
 
-        lax.fori_loop(0, layers, density, 0)
+        lax.fori_loop(0, size - 1, faces, 0)
 
-        def sweep_one(e, carry):
-            center = first[e]
-            remainder = dens[e] - applied(first, e)
-            direction = keep_one * center + mix_one * remainder
-            rem[e] = remainder
-            second[e] = direction
-            partial[e] = center + direction
-            return carry
+        for k in range(pairs):
+            weight = weight_ref[k]
 
-        lax.fori_loop(1, layers - 1, sweep_one, 0)
+            def density(e, carry):
+                own = psi_ref[0, start + e].astype(jnp.float32)
+                partner = psi_ref[k + 1, start + e].astype(jnp.float32)
+                value = (FOUR_PI * own) * partner
+                dens[e] = value
+                first[e] = value / CHEB_CENTER
+                return carry
 
-        def sweep_two(e, carry):
-            remainder = rem[e] - applied(second, e)
-            direction = keep_two * second[e] + mix_two * remainder
-            potential = partial[e] + direction
-            partner = psi_ref[k + 1, e].astype(jnp.float32)
-            out_ref[e - HALO] += (weight * potential) * partner
-            return carry
+            lax.fori_loop(0, size, density, 0)
 
-        lax.fori_loop(HALO, layers - HALO, sweep_two, 0)
+            def sweep_one(e, carry):
+                center = first[e]
+                remainder = dens[e] - applied(first, e)
+                direction = keep_one * center + mix_one * remainder
+                rem[e] = remainder
+                second[e] = direction
+                partial[e] = center + direction
+                return carry
+
+            flux[...] = face_z[0] * (first[1] - first[0])
+            lax.fori_loop(1, size - 1, sweep_one, 0)
+
+            def sweep_two(e, carry):
+                remainder = rem[e] - applied(second, e)
+                direction = keep_two * second[e] + mix_two * remainder
+                potential = partial[e] + direction
+                partner = psi_ref[k + 1, start + e].astype(jnp.float32)
+                out_ref[out_at + e - HALO] += (weight * potential) * partner
+                return carry
+
+            flux[...] = face_z[1] * (second[2] - second[1])
+            lax.fori_loop(HALO, size - HALO, sweep_two, 0)
+        out_at += size - 2 * HALO
     out_ref[...] = -out_ref[...]
 
 
-def solve(weights, wide, padded_diel):
-    layers, rows, cols = padded_diel.shape
-    pairs = wide.shape[0] - 1
-    full = jax.ShapeDtypeStruct((layers, rows, cols), jnp.float32)
+def solve(weights, psi, eps, windows):
+    _, rows, cols = eps.shape
+    pairs = psi.shape[0] - 1
+    widest = max(size for _, size in windows)
+    outputs = sum(size - 2 * HALO for _, size in windows)
+    work = sum(3 * size for _, size in windows)
     vmem = pltpu.VMEM
+    layer = (rows, cols)
     return pl.pallas_call(
-        solve_kernel,
-        out_shape=jax.ShapeDtypeStruct((layers - 2 * HALO, rows, cols), jnp.float32),
-        in_specs=[
-            pl.BlockSpec(memory_space=vmem),
-            pl.BlockSpec(memory_space=vmem),
-            pl.BlockSpec(memory_space=vmem),
-        ],
+        functools.partial(solve_kernel, tuple(windows)),
+        out_shape=jax.ShapeDtypeStruct((outputs,) + layer, jnp.float32),
+        in_specs=[pl.BlockSpec(memory_space=vmem)] * 3,
         out_specs=pl.BlockSpec(memory_space=vmem),
-        scratch_shapes=[vmem((layers - 1, rows, cols), jnp.float32)] + [vmem(full.shape, jnp.float32)] * 7,
+        scratch_shapes=[vmem((widest,) + layer, jnp.float32)] * 8 + [vmem(layer, jnp.float32)],
         compiler_params=pltpu.CompilerParams(vmem_limit_bytes=48 * 1024 * 1024),
         cost_estimate=pl.CostEstimate(
-            flops=pairs * 3 * layers * rows * cols * 30,
+            flops=pairs * work * rows * cols * 25,
             transcendentals=0,
-            bytes_accessed=wide.size * 2 + padded_diel.size * 4 + (layers - 2 * HALO) * rows * cols * 4,
+            bytes_accessed=psi.size * 2 + eps.size * 4 + outputs * rows * cols * 4,
         ),
-    )(weights, wide, padded_diel)
+    )(weights, psi, eps)
 
 
 def exchanged(x, axis, pairs_of):
@@ -170,8 +172,11 @@
         ]
     )
     stack = jnp.stack([psi, slab(swap), slab(outer), slab(far), slab(relay)])
+    inner = solve(weights, stack, dielectric, [(0, depth)])
     wide = z_halo(stack, 1, HALO)
-    return solve(weights, wide, padded_diel)[None]
+    edge = solve(weights, wide, padded_diel, [(0, 3 * HALO), (depth - HALO, 3 * HALO)])
+    totals = jnp.concatenate([edge[:HALO], inner, edge[HALO:]])
+    return totals[None]
 
 
 def solution(mesh):

time: 74.2 us -> 71 us (0.957)
  the two profiles are of different devices: /device:TPU:64 before, /device:TPU:6 now
where the time goes in v5:
time: 71 us; the launch traced here: 70.6 us
  starting transfers between devices  34.7 us (49%)
  Pallas kernels  18 us (25%)
  waiting for transfers between devices  10.3 us (15%)
  other arithmetic  5.72 us (8%)
  between operations  0.98 us (1%)
  local copies, waits for them, and re-layouts  0.93 us (1%)
    pallas_call x2, Pallas kernels, solve(): pl.pallas_call(functools.partial(solve_kernel, tuple(windows)), out_shape...  18 us
    ppermute x4, starting transfers between devices, shifted(): return lax.ppermute(x, axis, [(i, (i + by) % size) for i in range(size)])  17.5 us
    ppermute x4, starting transfers between devices, exchanged(): return lax.ppermute(x, axis, [(i, pairs_of(i) % size) for i in range(size)])  17.2 us
    ppermute x4, waiting for transfers between devices, exchanged(): return lax.ppermute(x, axis, [(i, pairs_of(i) % size) for i in range(size)])  10.3 us
    another operation x5, other arithmetic, on_device(): jnp.stack([jnp.where(odd, own_flags(0), sent_flags(swap, 0)), jnp.where(o...  2.58 us
  transfers between devices with their start and end apart: 8, of which 2 were waited for; matrix products, arithmetic and copies ran while one was open for 5% of the time, Pallas kernels for 11%

profile of v5, /device:TPU:6, one launch (start us, length us, event | category | flops | bytes accessed | tf_op | source)
XLA Modules:
  0.0 70.6 jit_solution(13361246024615291811)
XLA Ops:
  0.0 0.0 copy-start
  0.7 0.7 %fusion.9 = (f32[2,1,1]{0,2,1:T(1,128)S(1)}, bf16[2]{0:T(256)(128)(2,1)S(1)}) fusion(s32[2,1,1]{0,2,1:T(1,128)} %param.9), kind=kLoop, calls=%fused_computation.30 | loop fusion | flops 4 | bytes 20 | tf_op jit(solution)/shard_map/convert_element_type | solution.py:142
  1.5 1.1 %constant_dynamic-update-slice_fusion.4 = (bf16[5,8,128,128]{3,2,1,0:T(8,128)(2,1)S(1)}, bf16[1,8,128,128]{3,2,1,0:T(8,128)(2,1)S(1)}) fusion(bf16[1,8,128,128]{3,2,1,0:T(8,128)(2,1)} %param.6, bf16[]{:T(256)} %bitcast.1), kind=kLoop, calls=%fused_computation.9 | loop fusion | flops 524287 | bytes 786434
  2.6 0.2 pad_maximum_fusion.2
  2.8 1.9 %collective-permute-start = (bf16[1040,128]{1,0:T(8,128)(2,1)S(1)}, bf16[1040,128]{1,0:T(8,128)(2,1)S(1)}, u32[]{:S(2)}, u32[]{:S(2)}) collective-permute-start(bf16[1040,128]{1,0:T(8,128)(2,1)S(1)} %pad_maximum_fusion.2), channel_id=1, source_target_pairs={{0,4},{4,0},{8,12},{12,8},{16,20},{20,16},{24,28},{28,24},{32,36},... | collective-permute-start | bytes 798728 | tf_op jit(solution)/shard_map/ppermute | solution.py:135
  4.7 0.0 copy-done
  4.7 4.3 %collective-permute-start.6 = (f32[2,128,128]{2,1,0:T(8,128)S(1)}, f32[2,128,128]{2,1,0:T(8,128)S(1)}, u32[]{:S(2)}, u32[]{:S(2)}) collective-permute-start(f32[2,128,128]{2,1,0:T(8,128)S(1)} %get-tuple-element.19), channel_id=1, source_target_pairs={{0,1},{1,2},{2,3},{3,0},{4,5},{5,6},{6,7},{7,4},{8,9},{9,10},{10,1... | collective-permute-start | bytes 393224 | tf_op jit(solution)/shard_map/ppermute | solution.py:23
  9.0 5.5 %collective-permute-start.7 = (f32[2,128,128]{2,1,0:T(8,128)S(1)}, f32[2,128,128]{2,1,0:T(8,128)S(1)}, u32[]{:S(2)}, u32[]{:S(2)}) collective-permute-start(f32[2,128,128]{2,1,0:T(8,128)S(1)} %get-tuple-element.20), channel_id=1, source_target_pairs={{0,3},{1,0},{2,1},{3,2},{4,7},{5,4},{6,5},{7,6},{8,11},{9,8},{10,9... | collective-permute-start | bytes 393224 | tf_op jit(solution)/shard_map/ppermute | solution.py:23
  14.6 11.5 %collective-permute-start.1 = (bf16[1040,128]{1,0:T(8,128)(2,1)S(1)}, bf16[1040,128]{1,0:T(8,128)(2,1)S(1)}, u32[]{:S(2)}, u32[]{:S(2)}) collective-permute-start(bf16[1040,128]{1,0:T(8,128)(2,1)S(1)} %pad_maximum_fusion.2), channel_id=1, source_target_pairs={{0,508},{4,8},{8,4},{12,16},{16,12},{20,24},{24,20},{28,32},{32,28... | collective-permute-start | bytes 798728 | tf_op jit(solution)/shard_map/ppermute | solution.py:135
  26.0 1.9 %collective-permute-start.2 = (bf16[1040,128]{1,0:T(8,128)(2,1)S(1)}, bf16[1040,128]{1,0:T(8,128)(2,1)S(1)}, u32[]{:S(2)}, u32[]{:S(2)}) collective-permute-start(bf16[1040,128]{1,0:T(8,128)(2,1)S(1)} %pad_maximum_fusion.2), channel_id=1, source_target_pairs={{0,8},{4,508},{8,16},{12,4},{16,24},{20,12},{24,32},{28,20},{32,40... | collective-permute-start | bytes 798728 | tf_op jit(solution)/shard_map/ppermute | solution.py:135
  27.9 0.6 fusion.8
  28.6 0.0 collective-permute-done.6
  28.6 0.0 collective-permute-done.7
  28.6 0.1 pad_maximum_fusion.1.eps_ref
  28.6 0.0 collective-permute-done
  28.7 3.4 %collective-permute-done.1 = bf16[1040,128]{1,0:T(8,128)(2,1)S(1)} collective-permute-done((bf16[1040,128]{1,0:T(8,128)(2,1)S(1)}, bf16[1040,128]{1,0:T(8,128)(2,1)S(1)}, u32[]{:S(2)}, u32[]{:S(2)}) %collective-permute-start.1) | collective-permute-done | bytes 266272 | tf_op jit(solution)/shard_map/ppermute | solution.py:135
  32.2 1.9 %collective-permute-start.3 = (bf16[1040,128]{1,0:T(8,128)(2,1)S(1)}, bf16[1040,128]{1,0:T(8,128)(2,1)S(1)}, u32[]{:S(2)}, u32[]{:S(2)}) collective-permute-start(bf16[1040,128]{1,0:T(8,128)(2,1)S(1)} %collective-permute-done.1), channel_id=1, source_target_pairs={{0,4},{4,0},{8,12},{12,8},{16,20},{20,16},{24,28},{28,24},{32,36},... | collective-permute-start | bytes 798728 | tf_op jit(solution)/shard_map/ppermute | solution.py:135
  34.1 0.7 fusion.1
  34.8 0.7 fusion.2
  35.5 6.9 %collective-permute-done.2 = bf16[1040,128]{1,0:T(8,128)(2,1)S(1)} collective-permute-done((bf16[1040,128]{1,0:T(8,128)(2,1)S(1)}, bf16[1040,128]{1,0:T(8,128)(2,1)S(1)}, u32[]{:S(2)}, u32[]{:S(2)}) %collective-permute-start.2) | collective-permute-done | bytes 266272 | tf_op jit(solution)/shard_map/ppermute | solution.py:135
  42.4 0.6 fusion.3
  43.0 0.0 collective-permute-done.3
  43.2 1.9 %collective-permute-start.4 = (bf16[5,2,128,128]{3,2,1,0:T(8,128)(2,1)S(1)}, bf16[5,2,128,128]{3,2,1,0:T(8,128)(2,1)S(1)}, u32[]{:S(2)}, u32[]{:S(2)}) collective-permute-start(bf16[5,2,128,128]{3,2,1,0:T(8,128)(2,1)S(1)} %get-tuple-element.17), channel_id=1, source_target_pairs={{0,1},{1,2},{2,3},{3,0},{4,5},{5,6},{6,7},{7,4},{8,9},{9,10},{10,1... | collective-permute-start | bytes 983048 | tf_op jit(solution)/shard_map/ppermute | solution.py:23
  45.1 5.7 %collective-permute-start.5 = (bf16[5,2,128,128]{3,2,1,0:T(8,128)(2,1)S(1)}, bf16[5,2,128,128]{3,2,1,0:T(8,128)(2,1)S(1)}, u32[]{:S(2)}, u32[]{:S(2)}) collective-permute-start(bf16[5,2,128,128]{3,2,1,0:T(8,128)(2,1)S(1)} %get-tuple-element.18), channel_id=1, source_target_pairs={{0,3},{1,0},{2,1},{3,2},{4,7},{5,4},{6,5},{7,6},{8,11},{9,8},{10,9... | collective-permute-start | bytes 983048 | tf_op jit(solution)/shard_map/ppermute | solution.py:23
  50.8 0.6 fusion.4
  51.5 8.0 %shard_map.47 = f32[4,128,128]{2,1,0:T(8,128)S(1)} custom-call(f32[4,1,128]{2,1,0:T(1,128)S(1)} %pad_maximum_fusion.3.weight_ref, bf16[5,8,128,128]{3,2,1,0:T(8,128)(2,1)S(1)} %constant_dynamic-update-slice_fusion.psi_ref, f32[8,128,128]{2,1,0:T(8,128)S(1)} %copy-done), custom_call_target="tpu_custom_call" | custom-call | flops 39321600 | bytes 2097152 | tf_op jit(solution)/shard_map/pallas_call | solution.py:118
  59.5 0.0 collective-permute-done.4
  59.5 0.0 collective-permute-done.5
  59.5 0.2 pad_maximum_fusion.psi_ref
  59.8 9.9 %shard_map.46 = f32[4,128,128]{2,1,0:T(8,128)S(1)} custom-call(f32[4,1,128]{2,1,0:T(1,128)S(1)} %pad_maximum_fusion.3.weight_ref, bf16[5,12,128,128]{3,2,1,0:T(8,128)(2,1)S(1)} %pad_maximum_fusion.psi_ref, f32[12,128,128]{2,1,0:T(8,128)S(1)} %pad_maximum_fusion.1.eps_ref), custom_call_target="tpu_custom_call" | custom-call | flops 58982400 | bytes 3014656 | tf_op jit(solution)/shard_map/pallas_call | solution.py:118
  69.7 0.8 %maximum_bitcast_fusion = f32[1,8,128,128]{3,2,1,0:T(8,128)} fusion(f32[2,128,128]{2,1,0:T(8,128)S(1)} %get-tuple-element.22, f32[4,128,128]{2,1,0:T(8,128)S(1)} %shard_map.47, f32[2,128,128]{2,1,0:T(8,128)S(1)} %get-tuple-element.21), kind=kLoop, calls=%fused_computation.2 | loop fusion | flops 262144 | bytes 1048576 | tf_op jit(solution)/shard_map/broadcast_in_dim | solution.py:179
  (13 shorter events, 0.3 us)
Async XLA Ops:
  0.0 4.7 %copy-start = (f32[8,128,128]{2,1,0:T(8,128)S(1)}, f32[8,128,128]{2,1,0:T(8,128)}, u32[]{:S(2)}) copy-start(f32[8,128,128]{2,1,0:T(8,128)} %eps_ref.1) | copy-start | bytes 1572868
  2.8 25.9 %collective-permute-start = (bf16[1040,128]{1,0:T(8,128)(2,1)S(1)}, bf16[1040,128]{1,0:T(8,128)(2,1)S(1)}, u32[]{:S(2)}, u32[]{:S(2)}) collective-permute-start(bf16[1040,128]{1,0:T(8,128)(2,1)S(1)} %pad_maximum_fusion.2), channel_id=1, source_target_pairs={{0,4},{4,0},{8,12},{12,8},{16,20},{20,16},{24,28},{28,24},{32,36},... | collective-permute-start | bytes 798728 | tf_op jit(solution)/shard_map/ppermute | solution.py:135
  4.7 23.8 %collective-permute-start.6 = (f32[2,128,128]{2,1,0:T(8,128)S(1)}, f32[2,128,128]{2,1,0:T(8,128)S(1)}, u32[]{:S(2)}, u32[]{:S(2)}) collective-permute-start(f32[2,128,128]{2,1,0:T(8,128)S(1)} %get-tuple-element.19), channel_id=1, source_target_pairs={{0,1},{1,2},{2,3},{3,0},{4,5},{5,6},{6,7},{7,4},{8,9},{9,10},{10,1... | collective-permute-start | bytes 393224 | tf_op jit(solution)/shard_map/ppermute | solution.py:23
  9.0 19.6 %collective-permute-start.7 = (f32[2,128,128]{2,1,0:T(8,128)S(1)}, f32[2,128,128]{2,1,0:T(8,128)S(1)}, u32[]{:S(2)}, u32[]{:S(2)}) collective-permute-start(f32[2,128,128]{2,1,0:T(8,128)S(1)} %get-tuple-element.20), channel_id=1, source_target_pairs={{0,3},{1,0},{2,1},{3,2},{4,7},{5,4},{6,5},{7,6},{8,11},{9,8},{10,9... | collective-permute-start | bytes 393224 | tf_op jit(solution)/shard_map/ppermute | solution.py:23
  14.6 17.6 %collective-permute-start.1 = (bf16[1040,128]{1,0:T(8,128)(2,1)S(1)}, bf16[1040,128]{1,0:T(8,128)(2,1)S(1)}, u32[]{:S(2)}, u32[]{:S(2)}) collective-permute-start(bf16[1040,128]{1,0:T(8,128)(2,1)S(1)} %pad_maximum_fusion.2), channel_id=1, source_target_pairs={{0,508},{4,8},{8,4},{12,16},{16,12},{20,24},{24,20},{28,32},{32,28... | collective-permute-start | bytes 798728 | tf_op jit(solution)/shard_map/ppermute | solution.py:135
  26.0 16.3 %collective-permute-start.2 = (bf16[1040,128]{1,0:T(8,128)(2,1)S(1)}, bf16[1040,128]{1,0:T(8,128)(2,1)S(1)}, u32[]{:S(2)}, u32[]{:S(2)}) collective-permute-start(bf16[1040,128]{1,0:T(8,128)(2,1)S(1)} %pad_maximum_fusion.2), channel_id=1, source_target_pairs={{0,8},{4,508},{8,16},{12,4},{16,24},{20,12},{24,32},{28,20},{32,40... | collective-permute-start | bytes 798728 | tf_op jit(solution)/shard_map/ppermute | solution.py:135
  32.2 10.9 %collective-permute-start.3 = (bf16[1040,128]{1,0:T(8,128)(2,1)S(1)}, bf16[1040,128]{1,0:T(8,128)(2,1)S(1)}, u32[]{:S(2)}, u32[]{:S(2)}) collective-permute-start(bf16[1040,128]{1,0:T(8,128)(2,1)S(1)} %collective-permute-done.1), channel_id=1, source_target_pairs={{0,4},{4,0},{8,12},{12,8},{16,20},{20,16},{24,28},{28,24},{32,36},... | collective-permute-start | bytes 798728 | tf_op jit(solution)/shard_map/ppermute | solution.py:135
  43.2 16.3 %collective-permute-start.4 = (bf16[5,2,128,128]{3,2,1,0:T(8,128)(2,1)S(1)}, bf16[5,2,128,128]{3,2,1,0:T(8,128)(2,1)S(1)}, u32[]{:S(2)}, u32[]{:S(2)}) collective-permute-start(bf16[5,2,128,128]{3,2,1,0:T(8,128)(2,1)S(1)} %get-tuple-element.17), channel_id=1, source_target_pairs={{0,1},{1,2},{2,3},{3,0},{4,5},{5,6},{6,7},{7,4},{8,9},{9,10},{10,1... | collective-permute-start | bytes 983048 | tf_op jit(solution)/shard_map/ppermute | solution.py:23
  45.1 14.4 %collective-permute-start.5 = (bf16[5,2,128,128]{3,2,1,0:T(8,128)(2,1)S(1)}, bf16[5,2,128,128]{3,2,1,0:T(8,128)(2,1)S(1)}, u32[]{:S(2)}, u32[]{:S(2)}) collective-permute-start(bf16[5,2,128,128]{3,2,1,0:T(8,128)(2,1)S(1)} %get-tuple-element.18), channel_id=1, source_target_pairs={{0,3},{1,0},{2,1},{3,2},{4,7},{5,4},{6,5},{7,6},{8,11},{9,8},{10,9... | collective-permute-start | bytes 983048 | tf_op jit(solution)/shard_map/ppermute | solution.py:23

commit v6 on v5

--- a/solution.py
+++ b/solution.py
@@ -21,15 +21,6 @@
 def shifted(x, axis, by):
     size = lax.axis_size(axis)
     return lax.ppermute(x, axis, [(i, (i + by) % size) for i in range(size)])
-
-
-def z_halo(x, dim, width):
-    length = x.shape[dim]
-    last = lax.slice_in_dim(x, length - width, length, axis=dim)
-    leading = lax.slice_in_dim(x, 0, width, axis=dim)
-    before = shifted(last, "depth", 1)
-    after = shifted(leading, "depth", -1)
-    return jnp.concatenate([before, x, after], axis=dim)
 
 
 def solve_kernel(windows, weight_ref, psi_ref, eps_ref, out_ref, face_z, face_x, face_y, dens, first, rem, second, partial, flux):
@@ -140,7 +131,6 @@
     depth, rows, cols = psi.shape
     ticks = plan.shape[0]
     flags = plan.astype(jnp.float32).reshape(ticks)
-    padded_diel = z_halo(dielectric, 0, HALO)
 
     info = jnp.zeros((16, cols), jnp.bfloat16).at[:ticks, :].set(
         jnp.broadcast_to(plan.astype(jnp.bfloat16).reshape(ticks, 1), (ticks, cols))
@@ -173,7 +163,20 @@
     )
     stack = jnp.stack([psi, slab(swap), slab(outer), slab(far), slab(relay)])
     inner = solve(weights, stack, dielectric, [(0, depth)])
-    wide = z_halo(stack, 1, HALO)
+    lanes = (HALO, rows, cols)
+    tops = jnp.concatenate([stack[:, depth - HALO :].astype(jnp.float32).reshape(-1, rows, cols), dielectric[depth - HALO :]])
+    bottoms = jnp.concatenate([stack[:, :HALO].astype(jnp.float32).reshape(-1, rows, cols), dielectric[:HALO]])
+    with jax.named_scope("halo_up"):
+        before = shifted(tops, "depth", 1)
+    with jax.named_scope("halo_down"):
+        after = shifted(bottoms, "depth", -1)
+    slabs = stack.shape[0]
+
+    def orbital_part(h):
+        return h[: slabs * HALO].reshape((slabs,) + lanes).astype(jnp.bfloat16)
+
+    wide = jnp.concatenate([orbital_part(before), stack, orbital_part(after)], axis=1)
+    padded_diel = jnp.concatenate([before[slabs * HALO :], dielectric, after[slabs * HALO :]])
     edge = solve(weights, wide, padded_diel, [(0, 3 * HALO), (depth - HALO, 3 * HALO)])
     totals = jnp.concatenate([edge[:HALO], inner, edge[HALO:]])
     return totals[None]

time: 71 us -> 87.8 us (1.24)
  the two profiles are of different devices: /device:TPU:6 before, /device:TPU:1 now
where the time goes in v6:
time: 87.8 us; the launch traced here: 87.5 us
  starting transfers between devices  36.8 us (42%)
  waiting for transfers between devices  24.7 us (28%)
  Pallas kernels  18 us (21%)
  other arithmetic  5.98 us (7%)
  local copies, waits for them, and re-layouts  1.04 us (1%)
  between operations  1.01 us (1%)
    ppermute x4, starting transfers between devices, exchanged(): return lax.ppermute(x, axis, [(i, pairs_of(i) % size) for i in range(size)])  29.8 us
    ppermute x2, waiting for transfers between devices, shifted(): return lax.ppermute(x, axis, [(i, (i + by) % size) for i in range(size)])  22.3 us
    pallas_call x2, Pallas kernels, solve(): pl.pallas_call(functools.partial(solve_kernel, tuple(windows)), out_shape...  18 us
    ppermute x2, starting transfers between devices, shifted(): return lax.ppermute(x, axis, [(i, (i + by) % size) for i in range(size)])  6.98 us
    another operation x5, other arithmetic, on_device(): jnp.stack([jnp.where(odd, own_flags(0), sent_flags(swap, 0)), jnp.where(o...  2.59 us
    ppermute x4, waiting for transfers between devices, exchanged(): return lax.ppermute(x, axis, [(i, pairs_of(i) % size) for i in range(size)])  2.38 us
  transfers between devices with their start and end apart: 6, of which 4 were waited for; matrix products, arithmetic and copies ran while one was open for 4% of the time, Pallas kernels for 9%

profile of v6, /device:TPU:1, one launch (start us, length us, event | category | flops | bytes accessed | tf_op | source)
XLA Modules:
  0.0 87.5 jit_solution(7425917366960794529)
XLA Ops:
  0.7 0.7 fusion.9
  1.5 1.1 %constant_dynamic-update-slice_fusion.4 = (bf16[5,8,128,128]{3,2,1,0:T(8,128)(2,1)S(1)}, bf16[1,8,128,128]{3,2,1,0:T(8,128)(2,1)S(1)}) fusion(bf16[1,8,128,128]{3,2,1,0:T(8,128)(2,1)} %param.6, bf16[]{:T(256)} %bitcast.1), kind=kLoop, calls=%fused_computation.15 | loop fusion | flops 524287 | bytes 786434
  2.6 0.2 pad_maximum_fusion.4
  2.8 16.6 %collective-permute-start.2 = (bf16[1040,128]{1,0:T(8,128)(2,1)S(1)}, bf16[1040,128]{1,0:T(8,128)(2,1)S(1)}, u32[]{:S(2)}, u32[]{:S(2)}) collective-permute-start(bf16[1040,128]{1,0:T(8,128)(2,1)S(1)} %pad_maximum_fusion.4), channel_id=1, source_target_pairs={{0,8},{4,508},{8,16},{12,4},{16,24},{20,12},{24,32},{28,20},{32,40... | collective-permute-start | bytes 798728 | tf_op jit(solution)/shard_map/ppermute | solution.py:126
  19.3 1.9 %collective-permute-start.1 = (bf16[1040,128]{1,0:T(8,128)(2,1)S(1)}, bf16[1040,128]{1,0:T(8,128)(2,1)S(1)}, u32[]{:S(2)}, u32[]{:S(2)}) collective-permute-start(bf16[1040,128]{1,0:T(8,128)(2,1)S(1)} %pad_maximum_fusion.4), channel_id=1, source_target_pairs={{0,508},{4,8},{8,4},{12,16},{16,12},{20,24},{24,20},{28,32},{32,28... | collective-permute-start | bytes 798728 | tf_op jit(solution)/shard_map/ppermute | solution.py:126
  21.3 3.4 %collective-permute-start = (bf16[1040,128]{1,0:T(8,128)(2,1)S(1)}, bf16[1040,128]{1,0:T(8,128)(2,1)S(1)}, u32[]{:S(2)}, u32[]{:S(2)}) collective-permute-start(bf16[1040,128]{1,0:T(8,128)(2,1)S(1)} %pad_maximum_fusion.4), channel_id=1, source_target_pairs={{0,4},{4,0},{8,12},{12,8},{16,20},{20,16},{24,28},{28,24},{32,36},... | collective-permute-start | bytes 798728 | tf_op jit(solution)/shard_map/ppermute | solution.py:126
  24.6 0.0 copy-done
  24.7 0.6 fusion.8
  25.3 2.1 %collective-permute-done.1 = bf16[1040,128]{1,0:T(8,128)(2,1)S(1)} collective-permute-done((bf16[1040,128]{1,0:T(8,128)(2,1)S(1)}, bf16[1040,128]{1,0:T(8,128)(2,1)S(1)}, u32[]{:S(2)}, u32[]{:S(2)}) %collective-permute-start.1) | collective-permute-done | bytes 266272 | tf_op jit(solution)/shard_map/ppermute | solution.py:126
  27.4 8.0 %collective-permute-start.3 = (bf16[1040,128]{1,0:T(8,128)(2,1)S(1)}, bf16[1040,128]{1,0:T(8,128)(2,1)S(1)}, u32[]{:S(2)}, u32[]{:S(2)}) collective-permute-start(bf16[1040,128]{1,0:T(8,128)(2,1)S(1)} %collective-permute-done.1), channel_id=1, source_target_pairs={{0,4},{4,0},{8,12},{12,8},{16,20},{20,16},{24,28},{28,24},{32,36},... | collective-permute-start | bytes 798728 | tf_op jit(solution)/shard_map/ppermute | solution.py:126
  35.3 0.0 collective-permute-done
  35.5 0.0 collective-permute-done.2
  35.6 0.7 fusion.2
  36.2 0.3 collective-permute-done.3
  36.6 0.1 bitcast_convert_fusion.1
  36.7 0.1 bitcast_convert_fusion
  36.8 0.1 pad_maximum_fusion.2
  36.8 5.1 %collective-permute-start.5 = (f32[12,128,128]{2,1,0:T(8,128)S(1)}, f32[12,128,128]{2,1,0:T(8,128)S(1)}, u32[]{:S(2)}, u32[]{:S(2)}) collective-permute-start(f32[12,128,128]{2,1,0:T(8,128)S(1)} %pad_maximum_fusion.2), channel_id=1, source_target_pairs={{0,3},{1,0},{2,1},{3,2},{4,7},{5,4},{6,5},{7,6},{8,11},{9,8},{10,9... | collective-permute-start | bytes 2359304 | tf_op jit(solution)/shard_map/halo_down/ppermute | solution.py:23
  41.9 0.1 pad_maximum_fusion.1
  42.0 1.9 %collective-permute-start.4 = (f32[12,128,128]{2,1,0:T(8,128)S(1)}, f32[12,128,128]{2,1,0:T(8,128)S(1)}, u32[]{:S(2)}, u32[]{:S(2)}) collective-permute-start(f32[12,128,128]{2,1,0:T(8,128)S(1)} %pad_maximum_fusion.1), channel_id=1, source_target_pairs={{0,1},{1,2},{2,3},{3,0},{4,5},{5,6},{6,7},{7,4},{8,9},{9,10},{10,1... | collective-permute-start | bytes 2359304 | tf_op jit(solution)/shard_map/halo_up/ppermute | solution.py:23
  43.9 0.7 fusion.1
  44.5 0.6 fusion.3
  45.2 0.6 fusion.4
  45.8 8.0 %shard_map.47 = f32[4,128,128]{2,1,0:T(8,128)S(1)} custom-call(f32[4,1,128]{2,1,0:T(1,128)S(1)} %pad_maximum_fusion.5.weight_ref, bf16[5,8,128,128]{3,2,1,0:T(8,128)(2,1)S(1)} %constant_dynamic-update-slice_fusion.psi_ref, f32[8,128,128]{2,1,0:T(8,128)S(1)} %copy-done), custom_call_target="tpu_custom_call" | custom-call | flops 39321600 | bytes 2097152 | tf_op jit(solution)/shard_map/pallas_call | solution.py:109
  53.9 4.6 %collective-permute-done.5 = f32[12,128,128]{2,1,0:T(8,128)S(1)} collective-permute-done((f32[12,128,128]{2,1,0:T(8,128)S(1)}, f32[12,128,128]{2,1,0:T(8,128)S(1)}, u32[]{:S(2)}, u32[]{:S(2)}) %collective-permute-start.5) | collective-permute-done | bytes 786464 | tf_op jit(solution)/shard_map/halo_down/ppermute | solution.py:23
  58.5 0.1 slice.132
  58.5 17.7 %collective-permute-done.4 = f32[12,128,128]{2,1,0:T(8,128)S(1)} collective-permute-done((f32[12,128,128]{2,1,0:T(8,128)S(1)}, f32[12,128,128]{2,1,0:T(8,128)S(1)}, u32[]{:S(2)}, u32[]{:S(2)}) %collective-permute-start.4) | collective-permute-done | bytes 786464 | tf_op jit(solution)/shard_map/halo_up/ppermute | solution.py:23
  76.3 0.1 slice.133
  76.3 0.2 pad_maximum_fusion.psi_ref
  76.6 0.1 pad_maximum_fusion.3.eps_ref
  76.7 9.9 %shard_map.46 = f32[4,128,128]{2,1,0:T(8,128)S(1)} custom-call(f32[4,1,128]{2,1,0:T(1,128)S(1)} %pad_maximum_fusion.5.weight_ref, bf16[5,12,128,128]{3,2,1,0:T(8,128)(2,1)S(1)} %pad_maximum_fusion.psi_ref, f32[12,128,128]{2,1,0:T(8,128)S(1)} %pad_maximum_fusion.3.eps_ref), custom_call_target="tpu_custom_call" | custom-call | flops 58982400 | bytes 3014656 | tf_op jit(solution)/shard_map/pallas_call | solution.py:109
  86.6 0.8 maximum_bitcast_fusion
  (16 shorter events, 0.3 us)
Async XLA Ops:
  0.0 24.6 %copy-start = (f32[8,128,128]{2,1,0:T(8,128)S(1)}, f32[8,128,128]{2,1,0:T(8,128)}, u32[]{:S(2)}) copy-start(f32[8,128,128]{2,1,0:T(8,128)} %eps_ref.1) | copy-start | bytes 1572868
  2.8 32.7 %collective-permute-start.2 = (bf16[1040,128]{1,0:T(8,128)(2,1)S(1)}, bf16[1040,128]{1,0:T(8,128)(2,1)S(1)}, u32[]{:S(2)}, u32[]{:S(2)}) collective-permute-start(bf16[1040,128]{1,0:T(8,128)(2,1)S(1)} %pad_maximum_fusion.4), channel_id=1, source_target_pairs={{0,8},{4,508},{8,16},{12,4},{16,24},{20,12},{24,32},{28,20},{32,40... | collective-permute-start | bytes 798728 | tf_op jit(solution)/shard_map/ppermute | solution.py:126
  19.3 8.0 %collective-permute-start.1 = (bf16[1040,128]{1,0:T(8,128)(2,1)S(1)}, bf16[1040,128]{1,0:T(8,128)(2,1)S(1)}, u32[]{:S(2)}, u32[]{:S(2)}) collective-permute-start(bf16[1040,128]{1,0:T(8,128)(2,1)S(1)} %pad_maximum_fusion.4), channel_id=1, source_target_pairs={{0,508},{4,8},{8,4},{12,16},{16,12},{20,24},{24,20},{28,32},{32,28... | collective-permute-start | bytes 798728 | tf_op jit(solution)/shard_map/ppermute | solution.py:126
  21.3 14.1 %collective-permute-start = (bf16[1040,128]{1,0:T(8,128)(2,1)S(1)}, bf16[1040,128]{1,0:T(8,128)(2,1)S(1)}, u32[]{:S(2)}, u32[]{:S(2)}) collective-permute-start(bf16[1040,128]{1,0:T(8,128)(2,1)S(1)} %pad_maximum_fusion.4), channel_id=1, source_target_pairs={{0,4},{4,0},{8,12},{12,8},{16,20},{20,16},{24,28},{28,24},{32,36},... | collective-permute-start | bytes 798728 | tf_op jit(solution)/shard_map/ppermute | solution.py:126
  27.4 9.1 %collective-permute-start.3 = (bf16[1040,128]{1,0:T(8,128)(2,1)S(1)}, bf16[1040,128]{1,0:T(8,128)(2,1)S(1)}, u32[]{:S(2)}, u32[]{:S(2)}) collective-permute-start(bf16[1040,128]{1,0:T(8,128)(2,1)S(1)} %collective-permute-done.1), channel_id=1, source_target_pairs={{0,4},{4,0},{8,12},{12,8},{16,20},{20,16},{24,28},{28,24},{32,36},... | collective-permute-start | bytes 798728 | tf_op jit(solution)/shard_map/ppermute | solution.py:126
  36.8 21.7 %collective-permute-start.5 = (f32[12,128,128]{2,1,0:T(8,128)S(1)}, f32[12,128,128]{2,1,0:T(8,128)S(1)}, u32[]{:S(2)}, u32[]{:S(2)}) collective-permute-start(f32[12,128,128]{2,1,0:T(8,128)S(1)} %pad_maximum_fusion.2), channel_id=1, source_target_pairs={{0,3},{1,0},{2,1},{3,2},{4,7},{5,4},{6,5},{7,6},{8,11},{9,8},{10,9... | collective-permute-start | bytes 2359304 | tf_op jit(solution)/shard_map/halo_down/ppermute | solution.py:23
  42.0 34.3 %collective-permute-start.4 = (f32[12,128,128]{2,1,0:T(8,128)S(1)}, f32[12,128,128]{2,1,0:T(8,128)S(1)}, u32[]{:S(2)}, u32[]{:S(2)}) collective-permute-start(f32[12,128,128]{2,1,0:T(8,128)S(1)} %pad_maximum_fusion.1), channel_id=1, source_target_pairs={{0,1},{1,2},{2,3},{3,0},{4,5},{5,6},{6,7},{7,4},{8,9},{9,10},{10,1... | collective-permute-start | bytes 2359304 | tf_op jit(solution)/shard_map/halo_up/ppermute | solution.py:23

commit v7 on v5

--- a/solution.py
+++ b/solution.py
@@ -148,10 +148,10 @@
     message = jnp.concatenate(
         [(psi * occupied.astype(jnp.bfloat16)[0]).reshape(depth * rows, cols), info], axis=0
     )
-    swap = exchanged(message, "band", lambda b: b ^ 1)
     outer = exchanged(message, "band", lambda b: b + 1 if b % 2 else b - 1)
     far = exchanged(message, "band", lambda b: b - 2 if b % 2 else b + 2)
-    relay = exchanged(outer, "band", lambda b: b ^ 1)
+    both = exchanged(jnp.stack([message, outer]), "band", lambda b: b ^ 1)
+    swap, relay = both[0], both[1]
 
     def slab(m):
         return m[: depth * rows].reshape(depth, rows, cols)

time: 71 us -> 69.7 us (0.982)
  the two profiles are of different devices: /device:TPU:6 before, /device:TPU:56 now
where the time goes in v7:
time: 69.7 us; the launch traced here: 69.3 us
  starting transfers between devices  30.2 us (43%)
  Pallas kernels  18 us (26%)
  waiting for transfers between devices  13.6 us (20%)
  other arithmetic  5.78 us (8%)
  local copies, waits for them, and re-layouts  0.91 us (1%)
  between operations  0.91 us (1%)
    pallas_call x2, Pallas kernels, solve(): pl.pallas_call(functools.partial(solve_kernel, tuple(windows)), out_shape...  18 us
    ppermute x4, starting transfers between devices, shifted(): return lax.ppermute(x, axis, [(i, (i + by) % size) for i in range(size)])  16.2 us
    ppermute x3, starting transfers between devices, exchanged(): return lax.ppermute(x, axis, [(i, pairs_of(i) % size) for i in range(size)])  14 us
    ppermute x4, waiting for transfers between devices, shifted(): return lax.ppermute(x, axis, [(i, (i + by) % size) for i in range(size)])  13.6 us
  transfers between devices with their start and end apart: 7, of which 2 were waited for; matrix products, arithmetic and copies ran while one was open for 5% of the time, Pallas kernels for 12%

profile of v7, /device:TPU:56, one launch (start us, length us, event | category | flops | bytes accessed | tf_op | source)
XLA Modules:
  0.0 69.3 jit_solution(18008679960130773692)
XLA Ops:
  0.0 0.0 copy-start
  0.0 0.7 %fusion.9 = (f32[2,1,1]{0,2,1:T(1,128)S(1)}, bf16[2]{0:T(256)(128)(2,1)S(1)}) fusion(s32[2,1,1]{0,2,1:T(1,128)} %param.9), kind=kLoop, calls=%fused_computation.31 | loop fusion | flops 4 | bytes 20 | tf_op jit(solution)/shard_map/convert_element_type | solution.py:142
  1.4 1.1 %constant_dynamic-update-slice_fusion.4 = (bf16[5,8,128,128]{3,2,1,0:T(8,128)(2,1)S(1)}, bf16[1,8,128,128]{3,2,1,0:T(8,128)(2,1)S(1)}) fusion(bf16[1,8,128,128]{3,2,1,0:T(8,128)(2,1)} %param.6, bf16[]{:T(256)} %bitcast.1), kind=kLoop, calls=%fused_computation.10 | loop fusion | flops 524287 | bytes 786434
  2.5 0.2 fusion.3
  2.7 2.7 %collective-permute-start = (bf16[1040,128]{1,0:T(8,128)(2,1)S(1)}, bf16[1040,128]{1,0:T(8,128)(2,1)S(1)}, u32[]{:S(2)}, u32[]{:S(2)}) collective-permute-start(bf16[1040,128]{1,0:T(8,128)(2,1)S(1)} %get-tuple-element.26), channel_id=1, source_target_pairs={{0,508},{4,8},{8,4},{12,16},{16,12},{20,24},{24,20},{28,32},{32,28... | collective-permute-start | bytes 798728 | tf_op jit(solution)/shard_map/ppermute | solution.py:135
  5.4 9.3 %collective-permute-start.2 = (bf16[1040,128]{1,0:T(8,128)(2,1)S(1)}, bf16[1040,128]{1,0:T(8,128)(2,1)S(1)}, u32[]{:S(2)}, u32[]{:S(2)}) collective-permute-start(bf16[1040,128]{1,0:T(8,128)(2,1)S(1)} %get-tuple-element.26), channel_id=1, source_target_pairs={{0,8},{4,508},{8,16},{12,4},{16,24},{20,12},{24,32},{28,20},{32,40... | collective-permute-start | bytes 798728 | tf_op jit(solution)/shard_map/ppermute | solution.py:135
  14.8 0.0 copy-done
  14.8 7.2 %collective-permute-start.6 = (f32[2,128,128]{2,1,0:T(8,128)S(1)}, f32[2,128,128]{2,1,0:T(8,128)S(1)}, u32[]{:S(2)}, u32[]{:S(2)}) collective-permute-start(f32[2,128,128]{2,1,0:T(8,128)S(1)} %get-tuple-element.24), channel_id=1, source_target_pairs={{0,3},{1,0},{2,1},{3,2},{4,7},{5,4},{6,5},{7,6},{8,11},{9,8},{10,9... | collective-permute-start | bytes 393224 | tf_op jit(solution)/shard_map/ppermute | solution.py:23
  22.0 1.9 %collective-permute-start.5 = (f32[2,128,128]{2,1,0:T(8,128)S(1)}, f32[2,128,128]{2,1,0:T(8,128)S(1)}, u32[]{:S(2)}, u32[]{:S(2)}) collective-permute-start(f32[2,128,128]{2,1,0:T(8,128)S(1)} %get-tuple-element.23), channel_id=1, source_target_pairs={{0,1},{1,2},{2,3},{3,0},{4,5},{5,6},{6,7},{7,4},{8,9},{9,10},{10,1... | collective-permute-start | bytes 393224 | tf_op jit(solution)/shard_map/ppermute | solution.py:23
  23.9 0.6 fusion.8
  24.5 0.0 collective-permute-done
  24.5 0.1 pad_maximum_fusion.2
  24.6 1.9 %collective-permute-start.1 = (bf16[2,1040,128]{2,1,0:T(8,128)(2,1)S(1)}, bf16[2,1040,128]{2,1,0:T(8,128)(2,1)S(1)}, u32[]{:S(2)}, u32[]{:S(2)}) collective-permute-start(bf16[2,1040,128]{2,1,0:T(8,128)(2,1)S(1)} %pad_maximum_fusion.2), channel_id=1, source_target_pairs={{0,4},{4,0},{8,12},{12,8},{16,20},{20,16},{24,28},{28,24},{32,36},... | collective-permute-start | bytes 1597448 | tf_op jit(solution)/shard_map/ppermute | solution.py:135
  26.5 9.9 %collective-permute-done.6 = f32[2,128,128]{2,1,0:T(8,128)S(1)} collective-permute-done((f32[2,128,128]{2,1,0:T(8,128)S(1)}, f32[2,128,128]{2,1,0:T(8,128)S(1)}, u32[]{:S(2)}, u32[]{:S(2)}) %collective-permute-start.6) | collective-permute-done | bytes 131104 | tf_op jit(solution)/shard_map/ppermute | solution.py:23
  36.4 0.0 collective-permute-done.5
  36.4 0.1 pad_maximum_fusion.1.eps_ref
  36.5 0.0 collective-permute-done.2
  36.6 0.6 fusion.2
  37.2 0.7 fusion.1
  37.9 0.0 collective-permute-done.1
  38.1 5.2 %collective-permute-start.4 = (bf16[5,2,128,128]{3,2,1,0:T(8,128)(2,1)S(1)}, bf16[5,2,128,128]{3,2,1,0:T(8,128)(2,1)S(1)}, u32[]{:S(2)}, u32[]{:S(2)}) collective-permute-start(bf16[5,2,128,128]{3,2,1,0:T(8,128)(2,1)S(1)} %get-tuple-element.18), channel_id=1, source_target_pairs={{0,3},{1,0},{2,1},{3,2},{4,7},{5,4},{6,5},{7,6},{8,11},{9,8},{10,9... | collective-permute-start | bytes 983048 | tf_op jit(solution)/shard_map/ppermute | solution.py:23
  43.4 1.9 %collective-permute-start.3 = (bf16[5,2,128,128]{3,2,1,0:T(8,128)(2,1)S(1)}, bf16[5,2,128,128]{3,2,1,0:T(8,128)(2,1)S(1)}, u32[]{:S(2)}, u32[]{:S(2)}) collective-permute-start(bf16[5,2,128,128]{3,2,1,0:T(8,128)(2,1)S(1)} %get-tuple-element.17), channel_id=1, source_target_pairs={{0,1},{1,2},{2,3},{3,0},{4,5},{5,6},{6,7},{7,4},{8,9},{9,10},{10,1... | collective-permute-start | bytes 983048 | tf_op jit(solution)/shard_map/ppermute | solution.py:23
  45.3 1.3 %broadcast_select_fusion.3 = (f32[1,1,128]{2,1,0:T(1,128)S(1)}, f32[1,1,128]{2,1,0:T(1,128)S(1)}) fusion(pred[]{:T(512)S(6)} %eq.5, bf16[2,1040,128]{2,1,0:T(8,128)(2,1)S(1)} %collective-permute-done.1, f32[]{:T(128)} %bitcast, f32[]{:T(128)} %bitcast.7), kind=kLoop, calls=%fused_computation.17 | loop fusion | flops 512 | bytes 1545 | tf_op jit(solution)/shard_map/jit(_where)/select_n | solution.py:168
  46.6 8.0 %shard_map.47 = f32[4,128,128]{2,1,0:T(8,128)S(1)} custom-call(f32[4,1,128]{2,1,0:T(1,128)S(1)} %pad_maximum_fusion.4.weight_ref, bf16[5,8,128,128]{3,2,1,0:T(8,128)(2,1)S(1)} %constant_dynamic-update-slice_fusion.psi_ref, f32[8,128,128]{2,1,0:T(8,128)S(1)} %copy-done), custom_call_target="tpu_custom_call" | custom-call | flops 39321600 | bytes 2097152 | tf_op jit(solution)/shard_map/pallas_call | solution.py:118
  54.7 0.0 collective-permute-done.4
  54.7 3.6 %collective-permute-done.3 = bf16[5,2,128,128]{3,2,1,0:T(8,128)(2,1)S(1)} collective-permute-done((bf16[5,2,128,128]{3,2,1,0:T(8,128)(2,1)S(1)}, bf16[5,2,128,128]{3,2,1,0:T(8,128)(2,1)S(1)}, u32[]{:S(2)}, u32[]{:S(2)}) %collective-permute-start.3) | collective-permute-done | bytes 327712 | tf_op jit(solution)/shard_map/ppermute | solution.py:23
  58.3 0.2 pad_maximum_fusion.psi_ref
  58.5 9.9 %shard_map.46 = f32[4,128,128]{2,1,0:T(8,128)S(1)} custom-call(f32[4,1,128]{2,1,0:T(1,128)S(1)} %pad_maximum_fusion.4.weight_ref, bf16[5,12,128,128]{3,2,1,0:T(8,128)(2,1)S(1)} %pad_maximum_fusion.psi_ref, f32[12,128,128]{2,1,0:T(8,128)S(1)} %pad_maximum_fusion.1.eps_ref), custom_call_target="tpu_custom_call" | custom-call | flops 58982400 | bytes 3014656 | tf_op jit(solution)/shard_map/pallas_call | solution.py:118
  68.5 0.8 %maximum_bitcast_fusion = f32[1,8,128,128]{3,2,1,0:T(8,128)} fusion(f32[2,128,128]{2,1,0:T(8,128)S(1)} %get-tuple-element.28, f32[4,128,128]{2,1,0:T(8,128)S(1)} %shard_map.47, f32[2,128,128]{2,1,0:T(8,128)S(1)} %get-tuple-element.27), kind=kLoop, calls=%fused_computation.3 | loop fusion | flops 262144 | bytes 1048576 | tf_op jit(solution)/shard_map/broadcast_in_dim | solution.py:179
  (12 shorter events, 0.3 us)
Async XLA Ops:
  0.0 14.8 %copy-start = (f32[8,128,128]{2,1,0:T(8,128)S(1)}, f32[8,128,128]{2,1,0:T(8,128)}, u32[]{:S(2)}) copy-start(f32[8,128,128]{2,1,0:T(8,128)} %eps_ref.1) | copy-start | bytes 1572868
  2.7 21.8 %collective-permute-start = (bf16[1040,128]{1,0:T(8,128)(2,1)S(1)}, bf16[1040,128]{1,0:T(8,128)(2,1)S(1)}, u32[]{:S(2)}, u32[]{:S(2)}) collective-permute-start(bf16[1040,128]{1,0:T(8,128)(2,1)S(1)} %get-tuple-element.26), channel_id=1, source_target_pairs={{0,508},{4,8},{8,4},{12,16},{16,12},{20,24},{24,20},{28,32},{32,28... | collective-permute-start | bytes 798728 | tf_op jit(solution)/shard_map/ppermute | solution.py:135
  5.4 31.1 %collective-permute-start.2 = (bf16[1040,128]{1,0:T(8,128)(2,1)S(1)}, bf16[1040,128]{1,0:T(8,128)(2,1)S(1)}, u32[]{:S(2)}, u32[]{:S(2)}) collective-permute-start(bf16[1040,128]{1,0:T(8,128)(2,1)S(1)} %get-tuple-element.26), channel_id=1, source_target_pairs={{0,8},{4,508},{8,16},{12,4},{16,24},{20,12},{24,32},{28,20},{32,40... | collective-permute-start | bytes 798728 | tf_op jit(solution)/shard_map/ppermute | solution.py:135
  14.8 21.6 %collective-permute-start.6 = (f32[2,128,128]{2,1,0:T(8,128)S(1)}, f32[2,128,128]{2,1,0:T(8,128)S(1)}, u32[]{:S(2)}, u32[]{:S(2)}) collective-permute-start(f32[2,128,128]{2,1,0:T(8,128)S(1)} %get-tuple-element.24), channel_id=1, source_target_pairs={{0,3},{1,0},{2,1},{3,2},{4,7},{5,4},{6,5},{7,6},{8,11},{9,8},{10,9... | collective-permute-start | bytes 393224 | tf_op jit(solution)/shard_map/ppermute | solution.py:23
  22.0 14.5 %collective-permute-start.5 = (f32[2,128,128]{2,1,0:T(8,128)S(1)}, f32[2,128,128]{2,1,0:T(8,128)S(1)}, u32[]{:S(2)}, u32[]{:S(2)}) collective-permute-start(f32[2,128,128]{2,1,0:T(8,128)S(1)} %get-tuple-element.23), channel_id=1, source_target_pairs={{0,1},{1,2},{2,3},{3,0},{4,5},{5,6},{6,7},{7,4},{8,9},{9,10},{10,1... | collective-permute-start | bytes 393224 | tf_op jit(solution)/shard_map/ppermute | solution.py:23
  24.6 13.3 %collective-permute-start.1 = (bf16[2,1040,128]{2,1,0:T(8,128)(2,1)S(1)}, bf16[2,1040,128]{2,1,0:T(8,128)(2,1)S(1)}, u32[]{:S(2)}, u32[]{:S(2)}) collective-permute-start(bf16[2,1040,128]{2,1,0:T(8,128)(2,1)S(1)} %pad_maximum_fusion.2), channel_id=1, source_target_pairs={{0,4},{4,0},{8,12},{12,8},{16,20},{20,16},{24,28},{28,24},{32,36},... | collective-permute-start | bytes 1597448 | tf_op jit(solution)/shard_map/ppermute | solution.py:135
  38.1 16.5 %collective-permute-start.4 = (bf16[5,2,128,128]{3,2,1,0:T(8,128)(2,1)S(1)}, bf16[5,2,128,128]{3,2,1,0:T(8,128)(2,1)S(1)}, u32[]{:S(2)}, u32[]{:S(2)}) collective-permute-start(bf16[5,2,128,128]{3,2,1,0:T(8,128)(2,1)S(1)} %get-tuple-element.18), channel_id=1, source_target_pairs={{0,3},{1,0},{2,1},{3,2},{4,7},{5,4},{6,5},{7,6},{8,11},{9,8},{10,9... | collective-permute-start | bytes 983048 | tf_op jit(solution)/shard_map/ppermute | solution.py:23
  43.4 14.9 %collective-permute-start.3 = (bf16[5,2,128,128]{3,2,1,0:T(8,128)(2,1)S(1)}, bf16[5,2,128,128]{3,2,1,0:T(8,128)(2,1)S(1)}, u32[]{:S(2)}, u32[]{:S(2)}) collective-permute-start(bf16[5,2,128,128]{3,2,1,0:T(8,128)(2,1)S(1)} %get-tuple-element.17), channel_id=1, source_target_pairs={{0,1},{1,2},{2,3},{3,0},{4,5},{5,6},{6,7},{7,4},{8,9},{9,10},{10,1... | collective-permute-start | bytes 983048 | tf_op jit(solution)/shard_map/ppermute | solution.py:23
